TPU v7x, 32 devices: a whole 2x2x4 slice. The times are simulated.
32 devices in a mesh: groups: 2 (over y), dp: 4 (over z), tensor: 4 (over x, core).
Axes of the slice: x: 2, y: 2, z: 4, core: 2. Of those that a mesh axis runs over, the one named last changes fastest.
Arguments:
- inputs: bfloat16 [2048, 8192], P(('groups', 'dp'), 'tensor'), parts along dimension 0, may hold values from -6 to 6
- cotangent: bfloat16 [2048, 8192], P(('groups', 'dp'), 'tensor'), parts along dimension 0, may hold values from -6 to 6
- up_blocks: bfloat16 [256, 64, 3, 256], P('dp', 'tensor'), may hold values from -0.21875 to 0.21875
- down_blocks: bfloat16 [256, 64, 3, 256], P('dp', 'tensor'), may hold values from -0.15625 to 0.15625
- low_left: bfloat16 [128, 8192], P(None, 'tensor'), may hold values from -0.0625 to 0.0625
- low_right: bfloat16 [128, 16384], P(None, 'tensor'), may hold values from -0.5 to 0.5
- up_pattern: int32 [64, 3], P('tensor'), may hold values from 0 to 7
- down_pattern: int32 [64, 3], P('tensor'), may hold values from 0 to 7
Outputs:
- grad_input: bfloat16 [2048, 8192], P(('groups', 'dp'), 'tensor'), parts along dimension 0
- grad_up: float32 [512, 64, 3, 256], P(('groups', 'dp'), 'tensor'), parts along dimension 0
- grad_down: float32 [512, 64, 3, 256], P(('groups', 'dp'), 'tensor'), parts along dimension 0
- grad_left: float32 [256, 8192], P(('groups', 'dp'), 'tensor'), parts along dimension 0
- grad_right: float32 [256, 16384], P(('groups', 'dp'), 'tensor'), parts along dimension 0
There are 2 independent parts, one for each index of `groups`. A program takes and returns all parts, laid end to end along the dimension named above; an argument that names none is the same for every part. Nothing has to cross between parts.
Inputs may be any that keep to these rules, and one draw needn't show every extreme that they name: `up_pattern`: feature block within a slice of 8 blocks. `down_pattern`: feature block within a slice of 8 blocks.
All inputs are finite; a program needn't handle non-finite values.
Results may differ from a plain program's by a relative error of at most 0.02.
Values may be sent and summed in bfloat16 or wider, within the bound.
No kernel may reach another device: no remote copies, remote signals or barrier semaphores. Data moves between devices by JAX's collectives and lax.ppermute only.
A program may use at most 128 MiB of HBM per device.

v0:
```python
import math

import jax
import jax.numpy as jnp
from jax import lax
from jax.sharding import PartitionSpec as P

root_coef = 0.7978845608028654
cubic_coef = 0.044715


def swapped(block, axis, distance):
    count = lax.axis_size(axis)
    route = []
    for low in range(count):
        high = low | 1 << distance
        if high != low and high < count:
            route += [(low, high), (high, low)]
    return lax.ppermute(block, axis, route)


def gelu_pair(values):
    inner_arg = root_coef * (values + cubic_coef * values * values * values)
    tangent = jnp.tanh(inner_arg)
    forward = 0.5 * values * (1.0 + tangent)
    slopes = 0.5 * (1.0 + tangent) + 0.5 * values * (1.0 - tangent * tangent) * root_coef * (
        1.0 + 3.0 * cubic_coef * values * values
    )
    return (forward, slopes)


def pick_blocks(slices, pattern, block_size):
    picked = []
    for which_section, source in enumerate(slices):
        shaped = source.reshape(source.shape[0], -1, block_size)
        picked.append(jnp.take(shaped, pattern[:, which_section], axis=1))
    return jnp.stack(picked, axis=2)


def shards(
    inputs, cotangent, up_blocks, down_blocks, low_left, low_right, up_pattern, down_pattern
):
    tokens_here, width_here = inputs.shape
    block_size = up_blocks.shape[3]
    hidden_here = up_blocks.shape[1]
    section_count = up_blocks.shape[2]
    blocks_here = width_here // block_size
    dp_size = lax.axis_size("dp")
    inv_root = 1.0 / math.sqrt(tokens_here * dp_size)
    up_full, down_full = (
        lax.all_gather(up_blocks, "dp", axis=0, tiled=True),
        lax.all_gather(down_blocks, "dp", axis=0, tiled=True),
    )
    sources = [inputs] + [
        swapped(inputs, "tensor", level_bit) for level_bit in range(section_count - 1)
    ]
    selected = pick_blocks(sources, up_pattern, block_size)
    sparse = jnp.einsum("thsi,ihsj->thj", selected, up_full, preferred_element_type=jnp.float32)
    low_part = lax.dot_general(
        inputs, low_left, (((1,), (1,)), ((), ())), preferred_element_type=jnp.float32
    )
    low_sum = lax.psum(low_part.astype(jnp.bfloat16), "tensor")
    preact = sparse.reshape(tokens_here, -1) + jnp.dot(
        low_sum, low_right, preferred_element_type=jnp.float32
    )
    activated, slopes = gelu_pair(preact)
    hidden = activated.astype(jnp.bfloat16)
    picked = pick_blocks([cotangent] * section_count, down_pattern, block_size)
    grad_hidden = jnp.einsum(
        "thso,jhso->thj", picked, down_full, preferred_element_type=jnp.float32
    ).reshape(tokens_here, -1)
    grad_pre = (grad_hidden * slopes).astype(jnp.bfloat16)
    grad_blocks = grad_pre.reshape(tokens_here, hidden_here, block_size)
    slot_ids = jnp.arange(blocks_here, dtype=jnp.int32)

    def section_term(which_section):
        spread = jnp.einsum(
            "thj,ihj->thi",
            grad_blocks,
            up_full[:, :, which_section, :],
            preferred_element_type=jnp.float32,
        )
        placing = (up_pattern[:, which_section][:, None] == slot_ids[None, :]).astype(jnp.float32)
        return jnp.einsum("thi,hd->tdi", spread, placing).reshape(tokens_here, width_here)

    own_term = section_term(0)
    for level_bit in range(section_count - 1):
        outgoing = section_term(level_bit + 1).astype(jnp.bfloat16)
        own_term = own_term + swapped(outgoing, "tensor", level_bit).astype(jnp.float32)
    back_part = lax.dot_general(
        grad_pre, low_right, (((1,), (1,)), ((), ())), preferred_element_type=jnp.float32
    )
    back_low = lax.psum(back_part.astype(jnp.bfloat16), "tensor")
    grad_input = (
        own_term + jnp.dot(back_low, low_left, preferred_element_type=jnp.float32)
    ).astype(jnp.bfloat16)
    row_part = selected
    grad_up = lax.psum_scatter(
        (
            jnp.einsum("thsi,thj->ihsj", row_part, grad_blocks, preferred_element_type=jnp.float32)
            * inv_root
        ).astype(jnp.bfloat16),
        "dp",
        scatter_dimension=0,
        tiled=True,
    ).astype(jnp.float32)
    hidden_blocks = hidden.reshape(tokens_here, hidden_here, block_size)
    row_part = hidden_blocks
    grad_down = lax.psum_scatter(
        (
            jnp.einsum("thj,thso->jhso", row_part, picked, preferred_element_type=jnp.float32)
            * inv_root
        ).astype(jnp.bfloat16),
        "dp",
        scatter_dimension=0,
        tiled=True,
    ).astype(jnp.float32)
    row_part = back_low
    grad_left = lax.psum_scatter(
        (
            lax.dot_general(
                row_part, inputs, (((0,), (0,)), ((), ())), preferred_element_type=jnp.float32
            )
            * inv_root
        ).astype(jnp.bfloat16),
        "dp",
        scatter_dimension=0,
        tiled=True,
    ).astype(jnp.float32)
    row_part = low_sum
    grad_right = lax.psum_scatter(
        (
            lax.dot_general(
                row_part, grad_pre, (((0,), (0,)), ((), ())), preferred_element_type=jnp.float32
            )
            * inv_root
        ).astype(jnp.bfloat16),
        "dp",
        scatter_dimension=0,
        tiled=True,
    ).astype(jnp.float32)
    return (grad_input, grad_up, grad_down, grad_left, grad_right)


def solution(mesh):
    in_specs = (
        P(("groups", "dp"), "tensor"),
        P(("groups", "dp"), "tensor"),
        P("dp", "tensor", None, None),
        P("dp", "tensor", None, None),
        P(None, "tensor"),
        P(None, "tensor"),
        P("tensor", None),
        P("tensor", None),
    )
    out_specs = (
        P(("groups", "dp"), "tensor"),
        P(("groups", "dp"), "tensor", None, None),
        P(("groups", "dp"), "tensor", None, None),
        P(("groups", "dp"), "tensor"),
        P(("groups", "dp"), "tensor"),
    )
    return jax.shard_map(shards, mesh=mesh, in_specs=in_specs, out_specs=out_specs, check_vma=False)
```

profile of v0, /device:TPU:0, one launch (start us, length us, event | category | flops | bytes accessed | tf_op | source)
XLA Modules:
  0.0 590.4 jit_solution(4953019336405703996)
XLA Ops:
  8.1 3.2 copy.60
  11.3 3.2 copy.67
  15.2 3.0 collective-permute-start.1
  18.2 2.1 convolution_convert_fusion.1
  20.4 2.3 copy.56
  28.3 2.1 gather_fusion
  32.9 3.4 select_bitcast_fusion.5
  39.3 2.4 select_bitcast_fusion.3
  47.0 2.1 gather_fusion.4
  49.1 4.8 select_bitcast_fusion
  53.9 75.6 %all-gather.3.cloned.1.call-done = bf16[256,16,3,256]{3,0,2,1:T(8,128)(2,1)} async-done(((bf16[64,16,3,256]{3,0,2,1:T(8,128)(2,1)}), bf16[256,16,3,256]{3,0,2,1:T(8,128)(2,1)}) %all-gather.3.cloned.1.call-update) | async-done | bytes 6291472 | tf_op jit(solution)/shard_map/all_gather | solution.py:52
  129.5 7.9 %fusion.17 = f32[16,256,256,1]{1,2,3,0:T(8,128)} fusion(bf16[256,16,3,256]{3,0,2,1:T(8,128)(2,1)} %all-gather.3.cloned.1.call-done, bf16[256,16,1,256]{3,0,2,1:T(8,128)(2,1)S(1)} %copy-done.6, bf16[256,16,1,256]{3,0,2,1:T(8,128)(2,1)} %get-tuple-element.47, bf16[256,16,1,256]{3,0,2,1:T(8,128)(2,1)} %select_bitcast_fusion.5), kind=kOutput, calls=%fused_computation.32 | convolution fusion | flops 1616904192 | bytes 16777216 | tf_op jit(solution)/shard_map/thso,jhso->thj/dot_general | solution.py:69
  137.3 107.2 %all-gather.5.cloned.1.call-done = bf16[256,16,3,256]{3,0,2,1:T(8,128)(2,1)} async-done(((bf16[64,16,3,256]{3,0,2,1:T(8,128)(2,1)}), bf16[256,16,3,256]{3,0,2,1:T(8,128)(2,1)}) %all-gather.5.cloned.1.call-update) | async-done | bytes 6291472 | tf_op jit(solution)/shard_map/all_gather | solution.py:51
  244.6 8.8 %fusion.16 = f32[16,256,256,1]{1,2,3,0:T(8,128)} fusion(bf16[256,16,3,256]{3,0,2,1:T(8,128)(2,1)} %all-gather.5.cloned.1.call-done, bf16[256,16,1,256]{3,0,2,1:T(8,128)(2,1)} %get-tuple-element.48, bf16[256,16,1,256]{3,0,2,1:T(8,128)(2,1)} %get-tuple-element.49, bf16[256,16,1,256]{3,0,2,1:T(8,128)(2,1)} %select_bitcast_fusion.2), kind=kOutput, calls=%fused_computation.31 | convolution fusion | flops 1616904192 | bytes 16777216 | tf_op jit(solution)/shard_map/thsi,ihsj->thj/dot_general | solution.py:58
  253.4 5.7 copy.69
  259.1 5.7 copy.68
  264.8 6.7 %multiply_convert_fusion.2 = (bf16[256,4096]{1,0:T(8,128)(2,1)}, bf16[256,4096]{1,0:T(8,128)(2,1)S(1)}) fusion(f32[256,4096]{1,0:T(8,128)} %copy.69, f32[256,4096]{1,0:T(8,128)} %copy.68, bf16[256,128]{1,0:T(8,128)(2,1)} %all-reduce.3.cloned.1.call-done, bf16[128,4096]{1,0:T(8,128)(2,1)S(1)} %copy-done), kind=kOutput, calls=%fused_computation.30 | convolution fusion | flops 291504128 | bytes 13697024 | tf_op jit(solution)/shard_map/dot_general | solution.py:63
  272.9 29.5 %all-reduce.5.cloned.1.call-done = bf16[256,128]{1,0:T(8,128)(2,1)} async-done(((bf16[256,128]{1,0:T(8,128)(2,1)}), bf16[256,128]{1,0:T(8,128)(2,1)}) %all-reduce.5.cloned.1.call-update) | async-done | bytes 65552 | tf_op jit(solution)/shard_map/psum | solution.py:93
  302.4 2.4 fusion.18
  308.9 6.3 %fusion = bf16[256,16,3,256]{0,3,2,1:T(8,128)(2,1)} fusion(bf16[256,16,1,256]{3,0,2,1:T(8,128)(2,1)S(1)} %copy-done.9, bf16[256,16,1,256]{3,0,2,1:T(8,128)(2,1)S(1)} %copy-done.10, bf16[256,16,1,256]{3,0,2,1:T(8,128)(2,1)} %select_bitcast_fusion.2, bf16[256,16,256,1]{2,1,0,3:T(8,128)(2,1)S(1)} %bitcast.145), kind=kOutput, calls=%fused_computation.8 | convolution fusion | flops 1635778560 | bytes 14680064 | tf_op jit(solution)/shard_map/thsi,thj->ihsj/dot_general | solution.py:100
  315.2 9.1 %copy.77 = bf16[256,16,3,256]{3,1,2,0:T(8,128)(2,1)} copy(bf16[256,16,3,256]{0,3,2,1:T(8,128)(2,1)} %fusion) | data formatting | bytes 12582912 | tf_op jit(solution)/shard_map/convert_element_type | solution.py:102
  324.3 2.4 copy.95
  327.2 6.8 %fusion.1 = bf16[256,16,3,256]{0,3,2,1:T(8,128)(2,1)} fusion(bf16[256,16,1,256]{3,0,2,1:T(8,128)(2,1)S(1)} %copy-done.7, bf16[256,16,1,256]{3,0,2,1:T(8,128)(2,1)S(1)} %copy-done.8, bf16[256,16,1,256]{3,0,2,1:T(8,128)(2,1)} %select_bitcast_fusion.5, bf16[256,16,256,1]{2,1,0,3:T(8,128)(2,1)S(1)} %bitcast.144), kind=kOutput, calls=%fused_computation.9 | convolution fusion | flops 1623195648 | bytes 14680064 | tf_op jit(solution)/shard_map/thj,thso->jhso/dot_general | solution.py:111
  334.0 8.9 %copy.80 = bf16[256,16,3,256]{3,1,2,0:T(8,128)(2,1)} copy(bf16[256,16,3,256]{0,3,2,1:T(8,128)(2,1)} %fusion.1) | data formatting | bytes 12582912 | tf_op jit(solution)/shard_map/convert_element_type | solution.py:113
  343.0 2.4 convolution_bitcast_fusion
  347.2 2.3 convolution_bitcast_fusion.1
  351.2 2.4 convolution_bitcast_fusion.2
  355.7 14.6 %collective-permute-done.3 = bf16[256,2048]{1,0:T(8,128)(2,1)S(1)} collective-permute-done((bf16[256,2048]{1,0:T(8,128)(2,1)S(1)}, bf16[256,2048]{1,0:T(8,128)(2,1)S(1)}, u32[]{:S(2)}, u32[]{:S(2)}) %collective-permute-start.3) | collective-permute-done | bytes 1048608 | tf_op jit(solution)/shard_map/ppermute | solution.py:19
  375.3 90.7 %reduce-scatter.5.cloned.1.call-done = bf16[64,16,3,256]{3,1,2,0:T(8,128)(2,1)} async-done(((bf16[256,16,3,256]{3,1,2,0:T(8,128)(2,1)}), bf16[64,16,3,256]{3,1,2,0:T(8,128)(2,1)}) %reduce-scatter.5.cloned.1.call-update) | async-done | bytes 1572880 | tf_op jit(solution)/shard_map/reduce_scatter | solution.py:98
  466.0 3.6 convert_element_type.86
  469.6 109.9 %reduce-scatter.7.cloned.1.call-done = bf16[64,16,3,256]{3,1,2,0:T(8,128)(2,1)} async-done(((bf16[256,16,3,256]{3,1,2,0:T(8,128)(2,1)}), bf16[64,16,3,256]{3,1,2,0:T(8,128)(2,1)}) %reduce-scatter.7.cloned.1.call-update) | async-done | bytes 1572880 | tf_op jit(solution)/shard_map/reduce_scatter | solution.py:109
  579.5 3.5 convert_element_type.90
  (88 shorter events, 33.6 us)
Async XLA Ops:
  8.0 256.8 %copy-start = (bf16[128,4096]{1,0:T(8,128)(2,1)S(1)}, bf16[128,4096]{1,0:T(8,128)(2,1)}, u32[]{:S(2)}) copy-start(bf16[128,4096]{1,0:T(8,128)(2,1)} %param.15) | copy-start | bytes 3145732
  8.0 121.5 %all-gather.3.cloned.1.call-start = ((), (), s32[]{:S(2)}) async-start(), calls=%async_computation.4 | async-start | bytes 7864320 | tf_op jit(solution)/shard_map/all_gather | solution.py:52
  11.3 3.3 copy-start.2
  11.3 233.3 %all-gather.5.cloned.1.call-start = ((), (), s32[]{:S(2)}) async-start(), calls=%async_computation.5 | async-start | bytes 7864320 | tf_op jit(solution)/shard_map/all_gather | solution.py:51
  14.6 250.2 %all-reduce.3.cloned.1.call-start = ((), (), s32[]{:S(2)}) async-start(), calls=%async_computation.6 | async-start | bytes 131072 | tf_op jit(solution)/shard_map/psum | solution.py:62
  15.2 26.8 %collective-permute-start.1 = (bf16[256,2048]{0,1:T(8,128)(2,1)S(1)}, bf16[256,2048]{0,1:T(8,128)(2,1)}, u32[]{:S(2)}, u32[]{:S(2)}) collective-permute-start(bf16[256,2048]{0,1:T(8,128)(2,1)S(1)} %copy.61), channel_id=1, source_target_pairs={{0,2},{2,0},{1,3},{3,1},{4,6},{6,4},{5,7},{7,5},{8,10},{10,8},{9,1... | collective-permute-start | bytes 3145736 | tf_op jit(solution)/shard_map/ppermute | solution.py:19
  18.2 25.3 %collective-permute-start = (bf16[256,2048]{0,1:T(8,128)(2,1)S(1)}, bf16[256,2048]{0,1:T(8,128)(2,1)}, u32[]{:S(2)}, u32[]{:S(2)}) collective-permute-start(bf16[256,2048]{0,1:T(8,128)(2,1)S(1)} %copy.61), channel_id=1, source_target_pairs={{0,1},{1,0},{2,3},{3,2},{4,5},{5,4},{6,7},{7,6},{8,9},{9,8},{10,11... | collective-permute-start | bytes 3145736 | tf_op jit(solution)/shard_map/ppermute | solution.py:19
  20.3 3.9 copy-start.15
  20.3 282.1 %all-reduce.5.cloned.1.call-start = ((), (), s32[]{:S(2)}) async-start(), calls=%async_computation.7 | async-start | bytes 131072 | tf_op jit(solution)/shard_map/psum | solution.py:93
  28.3 2.1 copy-start.14
  32.9 3.4 copy-start.5
  36.3 2.4 copy-start.3
  36.3 3.0 copy-start.4
  49.1 80.4 %copy-start.6 = (bf16[256,16,1,256]{3,0,2,1:T(8,128)(2,1)S(1)}, bf16[256,16,1,256]{3,0,2,1:T(8,128)(2,1)}, u32[]{:S(2)}) copy-start(bf16[256,16,1,256]{3,0,2,1:T(8,128)(2,1)} %get-tuple-element.46) | copy-start | bytes 6291460
  271.5 33.4 %copy-start.13 = (bf16[256,128]{1,0:T(8,128)(2,1)S(1)}, bf16[256,128]{1,0:T(8,128)(2,1)}, u32[]{:S(2)}) copy-start(bf16[256,128]{1,0:T(8,128)(2,1)} %all-reduce.3.cloned.1.call-done) | copy-start | bytes 196612
  272.8 99.0 %reduce-scatter.9.cloned.1.call-start = ((), (), s32[]{:S(2)}) async-start(), calls=%async_computation.10 | async-start | bytes 655360 | tf_op jit(solution)/shard_map/reduce_scatter | solution.py:119
  304.8 68.7 %reduce-scatter.11.cloned.1.call-start = ((), (), s32[]{:S(2)}) async-start(), calls=%async_computation.11 | async-start | bytes 1310720 | tf_op jit(solution)/shard_map/reduce_scatter | solution.py:131
  306.4 159.6 %reduce-scatter.5.cloned.1.call-start = ((), (), s32[]{:S(2)}) async-start(), calls=%async_computation.8 | async-start | bytes 7864320 | tf_op jit(solution)/shard_map/reduce_scatter | solution.py:98
  306.6 1.6 copy-start.9
  306.6 2.2 copy-start.10
  324.2 255.2 %reduce-scatter.7.cloned.1.call-start = ((), (), s32[]{:S(2)}) async-start(), calls=%async_computation.9 | async-start | bytes 7864320 | tf_op jit(solution)/shard_map/reduce_scatter | solution.py:109
  324.3 2.4 copy-start.7
  324.3 2.9 copy-start.8
  347.0 23.4 %collective-permute-start.3 = (bf16[256,2048]{1,0:T(8,128)(2,1)S(1)}, bf16[256,2048]{1,0:T(8,128)(2,1)S(1)}, u32[]{:S(2)}, u32[]{:S(2)}) collective-permute-start(bf16[256,2048]{1,0:T(8,128)(2,1)S(1)} %bitcast.146), channel_id=1, source_target_pairs={{0,2},{2,0},{1,3},{3,1},{4,6},{6,4},{5,7},{7,5},{8,10},{10,8},{9,1... | collective-permute-start | bytes 3145736 | tf_op jit(solution)/shard_map/ppermute | solution.py:19
  351.1 19.2 %collective-permute-start.2 = (bf16[256,2048]{1,0:T(8,128)(2,1)S(1)}, bf16[256,2048]{1,0:T(8,128)(2,1)S(1)}, u32[]{:S(2)}, u32[]{:S(2)}) collective-permute-start(bf16[256,2048]{1,0:T(8,128)(2,1)S(1)} %bitcast.147), channel_id=1, source_target_pairs={{0,1},{1,0},{2,3},{3,2},{4,5},{5,4},{6,7},{7,6},{8,9},{9,8},{10,11... | collective-permute-start | bytes 3145736 | tf_op jit(solution)/shard_map/ppermute | solution.py:19
  354.8 15.5 %copy-start.11 = (bf16[128,2048]{1,0:T(8,128)(2,1)S(1)}, bf16[128,2048]{1,0:T(8,128)(2,1)}, u32[]{:S(2)}) copy-start(bf16[128,2048]{1,0:T(8,128)(2,1)} %param.14) | copy-start | bytes 1572868
  354.8 15.5 %copy-start.12 = (bf16[256,128]{1,0:T(8,128)(2,1)S(1)}, bf16[256,128]{1,0:T(8,128)(2,1)}, u32[]{:S(2)}) copy-start(bf16[256,128]{1,0:T(8,128)(2,1)} %all-reduce.5.cloned.1.call-done) | copy-start | bytes 196612
  466.0 117.0 %copy-start.1 = (bf16[128,4096]{1,0:T(8,128)(2,1)S(1)}, bf16[128,4096]{1,0:T(8,128)(2,1)}, u32[]{:S(2)}) copy-start(bf16[128,4096]{1,0:T(8,128)(2,1)} %param.15) | copy-start | bytes 3145732
Sparse Core Ops, SparseCore 0:
  11.4 118.0 all-gather.2
  131.0 113.4 all-gather.4
  305.0 21.8 reduce-scatter.8
  329.0 25.5 reduce-scatter.10
  356.7 109.2 reduce-scatter.4
  468.2 111.2 reduce-scatter.6
Sparse Core Ops, SparseCore 1:
  20.4 31.8 all-reduce.2
  272.9 29.4 all-reduce.4
where the time goes:
time: 592 us; the launch traced here: 590 us
  waiting for transfers between devices  428 us (72%)
  local copies, waits for them, and re-layouts  63.8 us (11%)
  matrix products  56.2 us (9%)
  other arithmetic  22.9 us (4%)
  between operations  15.9 us (3%)
    reduce_scatter x1, waiting for transfers between devices, shards(): lax.psum_scatter((jnp.einsum('thj,thso->jhso', row_part, picked, preferre...  110 us
    all_gather x1, waiting for transfers between devices, shards(): lax.all_gather(up_blocks, 'dp', axis=0, tiled=True)  107 us
    reduce_scatter x1, waiting for transfers between devices, shards(): lax.psum_scatter((jnp.einsum('thsi,thj->ihsj', row_part, grad_blocks, pre...  90.7 us
    all_gather x1, waiting for transfers between devices, shards(): lax.all_gather(down_blocks, 'dp', axis=0, tiled=True)  75.6 us
    psum x1, waiting for transfers between devices, shards(): back_low = lax.psum(back_part.astype(jnp.bfloat16), 'tensor')  29.5 us
    unnamed x41, local copies, waits for them, and re-layouts  17.2 us
    ppermute x4, waiting for transfers between devices, swapped(): return lax.ppermute(block, axis, route)  14.8 us
    another operation x4, other arithmetic, pick_blocks(): return jnp.stack(picked, axis=2)  12.3 us
  transfers between devices with their start and end apart: 12, of which 7 were waited for; matrix products, arithmetic and copies ran while one was open for 21% of the time, Pallas kernels for 0%

commit v1 on v0

v1 whole, which is shorter than its diff:
```python
import math

import jax
import jax.numpy as jnp
from jax import lax
from jax.sharding import PartitionSpec as P

root_coef = 0.7978845608028654
cubic_coef = 0.044715


def swapped(block, axis, distance):
    count = lax.axis_size(axis)
    route = []
    for low in range(count):
        high = low | 1 << distance
        if high != low and high < count:
            route += [(low, high), (high, low)]
    return lax.ppermute(block, axis, route)


def line_gather(block, axis):
    count = lax.axis_size(axis)
    if count == 1:
        return block
    if count > 8:
        return lax.all_gather(block, axis, axis=0, tiled=True)
    me = lax.axis_index(axis)
    from_left, from_right = [], []
    rightward = leftward = block
    for step in range(1, count):
        rightward = lax.ppermute(rightward, axis, [(i, i + 1) for i in range(step - 1, count - 1)])
        leftward = lax.ppermute(leftward, axis, [(i + 1, i) for i in range(0, count - step)])
        from_left.append(rightward)
        from_right.append(leftward)
    window = jnp.concatenate(from_left[::-1] + [block] + from_right, axis=0)
    rows = block.shape[0]
    return lax.dynamic_slice_in_dim(window, (count - 1 - me) * rows, count * rows, axis=0)


def gelu_pair(values):
    inner_arg = root_coef * (values + cubic_coef * values * values * values)
    tangent = jnp.tanh(inner_arg)
    forward = 0.5 * values * (1.0 + tangent)
    slopes = 0.5 * (1.0 + tangent) + 0.5 * values * (1.0 - tangent * tangent) * root_coef * (
        1.0 + 3.0 * cubic_coef * values * values
    )
    return (forward, slopes)


def pick_blocks(slices, pattern, block_size):
    picked = []
    for which_section, source in enumerate(slices):
        shaped = source.reshape(source.shape[0], -1, block_size)
        picked.append(jnp.take(shaped, pattern[:, which_section], axis=1))
    return jnp.stack(picked, axis=2)


def scatter_dp(parts, inv_root, after=None):
    narrow = (jnp.stack(parts) * inv_root).astype(jnp.bfloat16)
    if after is not None:
        narrow, _ = lax.optimization_barrier((narrow, after))
    return lax.psum_scatter(narrow, "dp", scatter_dimension=0, tiled=False).astype(jnp.float32)


def row_split(values, axis):
    count = lax.axis_size("dp")
    rows = values.shape[axis] // count
    return [lax.slice_in_dim(values, d * rows, (d + 1) * rows, axis=axis) for d in range(count)]


def shards(
    inputs, cotangent, up_blocks, down_blocks, low_left, low_right, up_pattern, down_pattern
):
    tokens_here, width_here = inputs.shape
    block_size = up_blocks.shape[3]
    hidden_here = up_blocks.shape[1]
    section_count = up_blocks.shape[2]
    blocks_here = width_here // block_size
    dp_size = lax.axis_size("dp")
    inv_root = 1.0 / math.sqrt(tokens_here * dp_size)
    chunk_count = 4 if hidden_here % 4 == 0 else 1
    per_chunk = hidden_here // chunk_count
    width_chunk = per_chunk * block_size

    sources = [inputs] + [
        swapped(inputs, "tensor", level_bit) for level_bit in range(section_count - 1)
    ]
    selected = pick_blocks(sources, up_pattern, block_size)
    picked = pick_blocks([cotangent] * section_count, down_pattern, block_size)
    low_part = lax.dot_general(
        inputs, low_left, (((1,), (1,)), ((), ())), preferred_element_type=jnp.float32
    )
    low_sum = lax.psum(low_part.astype(jnp.bfloat16), "tensor")
    slot_ids = jnp.arange(blocks_here, dtype=jnp.int32)

    terms = [None] * section_count
    back_part = None
    grad_pre_chunks, grad_up_chunks, grad_down_chunks = [], [], []
    for chunk in range(chunk_count):
        lo = chunk * per_chunk
        hi = lo + per_chunk
        up_full = line_gather(up_blocks[:, lo:hi], "dp")
        down_full = line_gather(down_blocks[:, lo:hi], "dp")
        selected_here = selected[:, lo:hi]
        picked_here = picked[:, lo:hi]
        sparse = jnp.einsum(
            "thsi,ihsj->thj", selected_here, up_full, preferred_element_type=jnp.float32
        )
        preact = sparse.reshape(tokens_here, -1) + jnp.dot(
            low_sum,
            low_right[:, lo * block_size : hi * block_size],
            preferred_element_type=jnp.float32,
        )
        activated, slopes = gelu_pair(preact)
        hidden = activated.astype(jnp.bfloat16)
        grad_hidden = jnp.einsum(
            "thso,jhso->thj", picked_here, down_full, preferred_element_type=jnp.float32
        ).reshape(tokens_here, -1)
        grad_pre = (grad_hidden * slopes).astype(jnp.bfloat16)
        grad_pre_chunks.append(grad_pre)
        grad_blocks = grad_pre.reshape(tokens_here, per_chunk, block_size)
        for which_section in range(section_count):
            spread = jnp.einsum(
                "thj,ihj->thi",
                grad_blocks,
                up_full[:, :, which_section, :],
                preferred_element_type=jnp.float32,
            )
            placing = (
                up_pattern[lo:hi, which_section][:, None] == slot_ids[None, :]
            ).astype(jnp.float32)
            term = jnp.einsum("thi,hd->tdi", spread, placing).reshape(tokens_here, width_here)
            terms[which_section] = term if terms[which_section] is None else terms[which_section] + term
        back_here = lax.dot_general(
            grad_pre,
            low_right[:, lo * block_size : hi * block_size],
            (((1,), (1,)), ((), ())),
            preferred_element_type=jnp.float32,
        )
        back_part = back_here if back_part is None else back_part + back_here
        grad_up_chunks.append(
            scatter_dp(
                [
                    jnp.einsum("thsi,thj->hsij", rows, grad_blocks, preferred_element_type=jnp.float32)
                    for rows in row_split(selected_here, 3)
                ],
                inv_root,
                grad_down_chunks[-1] if grad_down_chunks else None,
            )
        )
        hidden_blocks = hidden.reshape(tokens_here, per_chunk, block_size)
        grad_down_chunks.append(
            scatter_dp(
                [
                    jnp.einsum("thj,thso->hjso", rows, picked_here, preferred_element_type=jnp.float32)
                    for rows in row_split(hidden_blocks, 2)
                ],
                inv_root,
                grad_up_chunks[-1],
            )
        )

    own_term = terms[0]
    for level_bit in range(section_count - 1):
        outgoing = terms[level_bit + 1].astype(jnp.bfloat16)
        own_term = own_term + swapped(outgoing, "tensor", level_bit).astype(jnp.float32)
    back_low = lax.psum(back_part.astype(jnp.bfloat16), "tensor")
    grad_input = (
        own_term + jnp.dot(back_low, low_left, preferred_element_type=jnp.float32)
    ).astype(jnp.bfloat16)
    grad_pre_all = jnp.concatenate(grad_pre_chunks, axis=1)
    grad_up = jnp.transpose(jnp.concatenate(grad_up_chunks, axis=0), (2, 0, 1, 3))
    grad_down = jnp.transpose(jnp.concatenate(grad_down_chunks, axis=0), (1, 0, 2, 3))
    grad_left = scatter_dp(
        row_split(
            lax.dot_general(
                back_low, inputs, (((0,), (0,)), ((), ())), preferred_element_type=jnp.float32
            ),
            0,
        ),
        inv_root,
    )
    grad_right = scatter_dp(
        row_split(
            lax.dot_general(
                low_sum, grad_pre_all, (((0,), (0,)), ((), ())), preferred_element_type=jnp.float32
            ),
            0,
        ),
        inv_root,
    )
    return (grad_input, grad_up, grad_down, grad_left, grad_right)


def solution(mesh):
    in_specs = (
        P(("groups", "dp"), "tensor"),
        P(("groups", "dp"), "tensor"),
        P("dp", "tensor", None, None),
        P("dp", "tensor", None, None),
        P(None, "tensor"),
        P(None, "tensor"),
        P("tensor", None),
        P("tensor", None),
    )
    out_specs = (
        P(("groups", "dp"), "tensor"),
        P(("groups", "dp"), "tensor", None, None),
        P(("groups", "dp"), "tensor", None, None),
        P(("groups", "dp"), "tensor"),
        P(("groups", "dp"), "tensor"),
    )
    return jax.shard_map(shards, mesh=mesh, in_specs=in_specs, out_specs=out_specs, check_vma=False)
```

time: 592 us -> 738 us (1.25); the launches traced: 590 us -> 725 us
  waiting for transfers between devices: 428 us -> 202 us
  local copies, waits for them, and re-layouts: 63.8 us -> 205 us
  starting transfers between devices: 3.83 us -> 96.5 us
  matrix products: 56.2 us -> 137 us
  other arithmetic: 22.9 us -> 66.9 us
    all_gather x2 -> x0, waiting for transfers between devices: 183 us -> none  [the longest x1 107 us: shards(): lax.all_gather(up_blocks, 'dp', axis=0, tiled=True)]
    reduce_scatter x4 -> x10, waiting for transfers between devices: 201 us -> 64.9 us  [scatter_dp(): lax.psum_scatter(narrow, 'dp', scatter_dimension=0, tiled=False)]
    ppermute x0 -> x48, waiting for transfers between devices: none -> 135 us  [the longest x24 108 us: line_gather(): lax.ppermute(leftward, axis, [(i + 1, i) for i in range(0, count - step)])]
    ppermute x0 -> x48, starting transfers between devices: none -> 91 us  [the longest x24 59 us: line_gather(): lax.ppermute(rightward, axis, [(i, i + 1) for i in range(step - 1, count...]
    dot_general x14 -> x74, matrix products: 52.6 us -> 133 us  [the longest x16 31 us: shards(): jnp.einsum('thsi,thj->hsij', rows, grad_blocks, preferred_element_type=jn...]
    ppermute x0 -> x24, local copies, waits for them, and re-layouts: none -> 52.5 us  [the longest x12 26.2 us: line_gather(): lax.ppermute(rightward, axis, [(i, i + 1) for i in range(step - 1, count...]
    convert_element_type x4 -> x24, other arithmetic: 10.5 us -> 47.6 us  [the longest x10 18.4 us: scatter_dp(): lax.psum_scatter(narrow, 'dp', scatter_dimension=0, tiled=False)]
    concatenate x0 -> x8, local copies, waits for them, and re-layouts: none -> 36.5 us  [line_gather(): window = jnp.concatenate(from_left[::-1] + [block] + from_right, axis=0)]
  transfers between devices with their start and end apart: 12 -> 64, of which waited for: 7 -> 22; matrix products, arithmetic and copies ran while one was open for 21% -> 52% of each run, Pallas kernels for 0% -> 0%
where the time goes in v1:
time: 738 us; the launch traced here: 725 us
  local copies, waits for them, and re-layouts  205 us (28%)
  waiting for transfers between devices  202 us (27%)
  matrix products  137 us (19%)
  starting transfers between devices  96.5 us (13%)
  other arithmetic  66.9 us (9%)
  between operations  16 us (2%)
    ppermute x24, waiting for transfers between devices, line_gather(): lax.ppermute(leftward, axis, [(i + 1, i) for i in range(0, count - step)])  108 us
    reduce_scatter x10, waiting for transfers between devices, scatter_dp(): lax.psum_scatter(narrow, 'dp', scatter_dimension=0, tiled=False)  64.9 us
    ppermute x24, starting transfers between devices, line_gather(): lax.ppermute(rightward, axis, [(i, i + 1) for i in range(step - 1, count...  59 us
    unnamed x167, local copies, waits for them, and re-layouts  51 us
    concatenate x8, local copies, waits for them, and re-layouts, line_gather(): window = jnp.concatenate(from_left[::-1] + [block] + from_right, axis=0)  36.5 us
    ppermute x24, starting transfers between devices, line_gather(): lax.ppermute(leftward, axis, [(i + 1, i) for i in range(0, count - step)])  31.9 us
    dot_general x16, matrix products, shards(): jnp.einsum('thsi,thj->hsij', rows, grad_blocks, preferred_element_type=jn...  31 us
    dot_general x16, matrix products, shards(): jnp.einsum('thj,thso->hjso', rows, picked_here, preferred_element_type=jn...  29 us
  transfers between devices with their start and end apart: 64, of which 22 were waited for; matrix products, arithmetic and copies ran while one was open for 52% of the time, Pallas kernels for 0%

profile of v1, /device:TPU:0, one launch (start us, length us, event | category | flops | bytes accessed | tf_op | source)
XLA Modules:
  0.0 724.6 jit_solution(9144401827917378441)
XLA Ops:
  17.6 4.4 collective-permute-start
  28.5 5.3 collective-permute-start.6
  63.8 5.6 collective-permute-done.9
  107.5 7.9 %concatenate.33 = bf16[448,4,3,256]{0,3,2,1:T(8,128)(2,1)} concatenate(bf16[64,4,3,256]{0,3,2,1:T(8,128)(2,1)} %copy.260, bf16[64,4,3,256]{0,3,2,1:T(8,128)(2,1)} %copy.261, bf16[64,4,3,256]{0,3,2,1:T(8,128)(2,1)S(1)} %copy-done.28, bf16[64,4,3,256]{0,3,2,1:T(8,128)(2,1)S(1)} %copy-done.26, bf16[64,4,3,256]{0,3,2,1:T(8,128)(2,1)} %copy.263, bf16[64,4,3,256]{0,3,2,1:T(8,128)(2,1)} %copy.264, ...), dimensions={0} | concatenate | bytes 5505024 | tf_op jit(solution)/shard_map/concatenate | solution.py:36
  140.3 7.5 %collective-permute-start.14 = (bf16[64,4,3,256]{3,0,2,1:T(8,128)(2,1)S(1)}, bf16[64,4,3,256]{3,0,2,1:T(8,128)(2,1)S(1)}, u32[]{:S(2)}, u32[]{:S(2)}) collective-permute-start(bf16[64,4,3,256]{3,0,2,1:T(8,128)(2,1)S(1)} %copy.283), channel_id=1, source_target_pairs={{0,4},{4,8},{8,12},{1,5},{5,9},{9,13},{2,6},{6,10},{10,14},{3,7},{... | collective-permute-start | bytes 1179656 | tf_op jit(solution)/shard_map/ppermute | solution.py:32
  149.2 6.0 collective-permute-start.20
  156.5 7.4 %collective-permute-done.14 = bf16[64,4,3,256]{3,0,2,1:T(8,128)(2,1)S(1)} collective-permute-done((bf16[64,4,3,256]{3,0,2,1:T(8,128)(2,1)S(1)}, bf16[64,4,3,256]{3,0,2,1:T(8,128)(2,1)S(1)}, u32[]{:S(2)}, u32[]{:S(2)}) %collective-permute-start.14) | collective-permute-done | bytes 393248 | tf_op jit(solution)/shard_map/ppermute | solution.py:32
  165.4 10.9 %collective-permute-done.17 = bf16[64,4,3,256]{3,0,2,1:T(8,128)(2,1)S(1)} collective-permute-done((bf16[64,4,3,256]{3,0,2,1:T(8,128)(2,1)S(1)}, bf16[64,4,3,256]{3,0,2,1:T(8,128)(2,1)S(1)}, u32[]{:S(2)}, u32[]{:S(2)}) %collective-permute-start.17) | collective-permute-done | bytes 393248 | tf_op jit(solution)/shard_map/ppermute | solution.py:33
  179.8 15.7 %collective-permute-done.23 = bf16[64,4,3,256]{3,0,2,1:T(8,128)(2,1)} collective-permute-done((bf16[64,4,3,256]{3,0,2,1:T(8,128)(2,1)S(1)}, bf16[64,4,3,256]{3,0,2,1:T(8,128)(2,1)}, u32[]{:S(2)}, u32[]{:S(2)}) %collective-permute-start.23) | collective-permute-done | bytes 393248 | tf_op jit(solution)/shard_map/ppermute | solution.py:33
  198.2 5.7 collective-permute-done.18
  236.1 7.9 %concatenate.35 = bf16[448,4,3,256]{0,3,2,1:T(8,128)(2,1)} concatenate(bf16[64,4,3,256]{0,3,2,1:T(8,128)(2,1)} %copy.285, bf16[64,4,3,256]{0,3,2,1:T(8,128)(2,1)} %copy.286, bf16[64,4,3,256]{0,3,2,1:T(8,128)(2,1)} %copy.287, bf16[64,4,3,256]{0,3,2,1:T(8,128)(2,1)} %copy.513, bf16[64,4,3,256]{0,3,2,1:T(8,128)(2,1)} %copy.288, bf16[64,4,3,256]{0,3,2,1:T(8,128)(2,1)} %copy.289, ...), dimensions={0} | concatenate | bytes 5505024 | tf_op jit(solution)/shard_map/concatenate | solution.py:36
  244.1 3.8 fusion.21
  255.6 4.3 collective-permute-done.25
  283.6 4.6 collective-permute-start.32
  289.5 9.5 %collective-permute-done.26 = bf16[64,4,3,256]{3,0,2,1:T(8,128)(2,1)S(1)} collective-permute-done((bf16[64,4,3,256]{3,0,2,1:T(8,128)(2,1)S(1)}, bf16[64,4,3,256]{3,0,2,1:T(8,128)(2,1)S(1)}, u32[]{:S(2)}, u32[]{:S(2)}) %collective-permute-start.26) | collective-permute-done | bytes 393248 | tf_op jit(solution)/shard_map/ppermute | solution.py:32
  300.4 10.4 %collective-permute-done.29 = bf16[64,4,3,256]{3,0,2,1:T(8,128)(2,1)S(1)} collective-permute-done((bf16[64,4,3,256]{3,0,2,1:T(8,128)(2,1)S(1)}, bf16[64,4,3,256]{3,0,2,1:T(8,128)(2,1)S(1)}, u32[]{:S(2)}, u32[]{:S(2)}) %collective-permute-start.29) | collective-permute-done | bytes 393248 | tf_op jit(solution)/shard_map/ppermute | solution.py:33
  315.2 14.1 %collective-permute-done.35 = bf16[64,4,3,256]{3,0,2,1:T(8,128)(2,1)} collective-permute-done((bf16[64,4,3,256]{3,0,2,1:T(8,128)(2,1)S(1)}, bf16[64,4,3,256]{3,0,2,1:T(8,128)(2,1)}, u32[]{:S(2)}, u32[]{:S(2)}) %collective-permute-start.35) | collective-permute-done | bytes 393248 | tf_op jit(solution)/shard_map/ppermute | solution.py:33
  332.0 5.7 collective-permute-done.30
  369.6 7.9 %concatenate.37 = bf16[448,4,3,256]{0,3,2,1:T(8,128)(2,1)} concatenate(bf16[64,4,3,256]{0,3,2,1:T(8,128)(2,1)} %copy.300, bf16[64,4,3,256]{0,3,2,1:T(8,128)(2,1)} %copy.301, bf16[64,4,3,256]{0,3,2,1:T(8,128)(2,1)} %copy.302, bf16[64,4,3,256]{0,3,2,1:T(8,128)(2,1)} %copy.515, bf16[64,4,3,256]{0,3,2,1:T(8,128)(2,1)} %copy.303, bf16[64,4,3,256]{0,3,2,1:T(8,128)(2,1)} %copy.304, ...), dimensions={0} | concatenate | bytes 5505024 | tf_op jit(solution)/shard_map/concatenate | solution.py:36
  377.6 3.8 fusion.19
  389.2 4.6 collective-permute-done.37
  418.7 4.6 collective-permute-start.44
  424.6 7.7 %collective-permute-done.38 = bf16[64,4,3,256]{3,0,2,1:T(8,128)(2,1)} collective-permute-done((bf16[64,4,3,256]{3,0,2,1:T(8,128)(2,1)S(1)}, bf16[64,4,3,256]{3,0,2,1:T(8,128)(2,1)}, u32[]{:S(2)}, u32[]{:S(2)}) %collective-permute-start.38) | collective-permute-done | bytes 393248 | tf_op jit(solution)/shard_map/ppermute | solution.py:32
  433.7 13.7 %collective-permute-done.41 = bf16[64,4,3,256]{3,0,2,1:T(8,128)(2,1)} collective-permute-done((bf16[64,4,3,256]{3,0,2,1:T(8,128)(2,1)S(1)}, bf16[64,4,3,256]{3,0,2,1:T(8,128)(2,1)}, u32[]{:S(2)}, u32[]{:S(2)}) %collective-permute-start.41) | collective-permute-done | bytes 393248 | tf_op jit(solution)/shard_map/ppermute | solution.py:33
  451.5 11.9 %collective-permute-done.47 = bf16[64,4,3,256]{3,0,2,1:T(8,128)(2,1)} collective-permute-done((bf16[64,4,3,256]{3,0,2,1:T(8,128)(2,1)}, bf16[64,4,3,256]{3,0,2,1:T(8,128)(2,1)}, u32[]{:S(2)}, u32[]{:S(2)}) %collective-permute-start.47) | collective-permute-done | bytes 393248 | tf_op jit(solution)/shard_map/ppermute | solution.py:33
  466.0 5.7 collective-permute-done.42
  494.0 7.8 %concatenate.39 = bf16[448,4,3,256]{0,3,2,1:T(8,128)(2,1)} concatenate(bf16[64,4,3,256]{0,3,2,1:T(8,128)(2,1)} %copy.315, bf16[64,4,3,256]{0,3,2,1:T(8,128)(2,1)} %copy.316, bf16[64,4,3,256]{0,3,2,1:T(8,128)(2,1)} %copy.317, bf16[64,4,3,256]{0,3,2,1:T(8,128)(2,1)S(1)} %copy-done.27, bf16[64,4,3,256]{0,3,2,1:T(8,128)(2,1)} %copy.318, bf16[64,4,3,256]{0,3,2,1:T(8,128)(2,1)} %copy.319, ...), dimensions={0} | concatenate | bytes 5505024 | tf_op jit(solution)/shard_map/concatenate | solution.py:36
  642.4 6.1 reduce-scatter.27.cloned.1.call-done
  650.2 26.4 %reduce-scatter.29.cloned.1.call-done = bf16[1,32,4096]{2,1,0:T(8,128)(2,1)} async-done(((bf16[4,32,4096]{2,1,0:T(8,128)(2,1)}), bf16[1,32,4096]{2,1,0:T(8,128)(2,1)}) %reduce-scatter.29.cloned.1.call-update) | async-done | bytes 262160 | tf_op jit(solution)/shard_map/reduce_scatter | solution.py:63
  679.7 3.5 copy.399
  683.2 29.5 %reduce-scatter.25.cloned.1.call-done = bf16[1,4,64,3,256]{4,2,3,1,0:T(8,128)(2,1)} async-done(((bf16[4,4,64,3,256]{4,2,3,1,0:T(8,128)(2,1)}), bf16[1,4,64,3,256]{4,2,3,1,0:T(8,128)(2,1)}) %reduce-scatter.25.cloned.1.call-update) | async-done | bytes 393232 | tf_op jit(solution)/shard_map/reduce_scatter | solution.py:63
  714.0 3.5 copy.400
  (469 shorter events, 435.2 us)
Async XLA Ops:
  7.2 66.2 %all-reduce.3.cloned.1.call-start = ((), (), s32[]{:S(2)}) async-start(), calls=%async_computation.10 | async-start | bytes 131072 | tf_op jit(solution)/shard_map/psum | solution.py:94
  9.6 78.9 %collective-permute-start.12 = (bf16[256,2048]{0,1:T(8,128)(2,1)}, bf16[256,2048]{0,1:T(8,128)(2,1)}, u32[]{:S(2)}, u32[]{:S(2)}) collective-permute-start(bf16[256,2048]{0,1:T(8,128)(2,1)} %copy.271), channel_id=1, source_target_pairs={{0,1},{1,0},{2,3},{3,2},{4,5},{5,4},{6,7},{7,6},{8,9},{9,8},{10,11... | collective-permute-start | bytes 3145736 | tf_op jit(solution)/shard_map/ppermute | solution.py:19
  10.1 81.4 %collective-permute-start.13 = (bf16[256,2048]{0,1:T(8,128)(2,1)}, bf16[256,2048]{0,1:T(8,128)(2,1)}, u32[]{:S(2)}, u32[]{:S(2)}) collective-permute-start(bf16[256,2048]{0,1:T(8,128)(2,1)} %copy.271), channel_id=1, source_target_pairs={{0,2},{2,0},{1,3},{3,1},{4,6},{6,4},{5,7},{7,5},{8,10},{10,8},{9,1... | collective-permute-start | bytes 3145736 | tf_op jit(solution)/shard_map/ppermute | solution.py:19
  17.6 38.9 %collective-permute-start = (bf16[64,4,3,256]{3,0,2,1:T(8,128)(2,1)}, bf16[64,4,3,256]{3,0,2,1:T(8,128)(2,1)}, u32[]{:S(2)}, u32[]{:S(2)}) collective-permute-start(bf16[64,4,3,256]{3,0,2,1:T(8,128)(2,1)} %copy.258), channel_id=1, source_target_pairs={{0,4},{4,8},{8,12},{1,5},{5,9},{9,13},{2,6},{6,10},{10,14},{3,7},{... | collective-permute-start | bytes 1179656 | tf_op jit(solution)/shard_map/ppermute | solution.py:32
  21.9 36.0 %collective-permute-start.3 = (bf16[64,4,3,256]{3,0,2,1:T(8,128)(2,1)}, bf16[64,4,3,256]{3,0,2,1:T(8,128)(2,1)}, u32[]{:S(2)}, u32[]{:S(2)}) collective-permute-start(bf16[64,4,3,256]{3,0,2,1:T(8,128)(2,1)} %copy.258), channel_id=1, source_target_pairs={{4,0},{8,4},{12,8},{5,1},{9,5},{13,9},{6,2},{10,6},{14,10},{7,3},{... | collective-permute-start | bytes 1179656 | tf_op jit(solution)/shard_map/ppermute | solution.py:33
  24.3 190.9 %reduce-scatter.11.cloned.1.call-start = ((), (), s32[]{:S(2)}) async-start(), calls=%async_computation.12 | async-start | bytes 1966080 | tf_op jit(solution)/shard_map/reduce_scatter | solution.py:63
  28.5 34.0 %collective-permute-start.6 = (bf16[64,4,3,256]{3,0,2,1:T(8,128)(2,1)}, bf16[64,4,3,256]{3,0,2,1:T(8,128)(2,1)}, u32[]{:S(2)}, u32[]{:S(2)}) collective-permute-start(bf16[64,4,3,256]{3,0,2,1:T(8,128)(2,1)} %copy.512), channel_id=1, source_target_pairs={{0,4},{4,8},{8,12},{1,5},{5,9},{9,13},{2,6},{6,10},{10,14},{3,7},{... | collective-permute-start | bytes 1179656 | tf_op jit(solution)/shard_map/ppermute | solution.py:32
  87.1 32.4 %collective-permute-start.8 = (bf16[64,4,3,256]{3,0,2,1:T(8,128)(2,1)}, bf16[64,4,3,256]{3,0,2,1:T(8,128)(2,1)}, u32[]{:S(2)}, u32[]{:S(2)}) collective-permute-start(bf16[64,4,3,256]{3,0,2,1:T(8,128)(2,1)} %collective-permute-done.7), channel_id=1, source_target_pairs={{8,12},{9,13},{10,14},{11,15},{24,28},{25,29},{26,30},{27,31}} | collective-permute-start | bytes 1179656 | tf_op jit(solution)/shard_map/ppermute | solution.py:32
  88.6 35.2 %collective-permute-start.11 = (bf16[64,4,3,256]{3,0,2,1:T(8,128)(2,1)}, bf16[64,4,3,256]{3,0,2,1:T(8,128)(2,1)}, u32[]{:S(2)}, u32[]{:S(2)}) collective-permute-start(bf16[64,4,3,256]{3,0,2,1:T(8,128)(2,1)} %collective-permute-done.10), channel_id=1, source_target_pairs={{4,0},{5,1},{6,2},{7,3},{20,16},{21,17},{22,18},{23,19}} | collective-permute-start | bytes 1179656 | tf_op jit(solution)/shard_map/ppermute | solution.py:33
  140.2 138.2 %reduce-scatter.13.cloned.1.call-start = ((), (), s32[]{:S(2)}) async-start(), calls=%async_computation.13 | async-start | bytes 1966080 | tf_op jit(solution)/shard_map/reduce_scatter | solution.py:63
  155.3 40.2 %collective-permute-start.23 = (bf16[64,4,3,256]{3,0,2,1:T(8,128)(2,1)S(1)}, bf16[64,4,3,256]{3,0,2,1:T(8,128)(2,1)}, u32[]{:S(2)}, u32[]{:S(2)}) collective-permute-start(bf16[64,4,3,256]{3,0,2,1:T(8,128)(2,1)S(1)} %copy.514), channel_id=1, source_target_pairs={{4,0},{8,4},{12,8},{5,1},{9,5},{13,9},{6,2},{10,6},{14,10},{7,3},{... | collective-permute-start | bytes 1179656 | tf_op jit(solution)/shard_map/ppermute | solution.py:33
  164.0 32.8 %collective-permute-start.15 = (bf16[64,4,3,256]{3,0,2,1:T(8,128)(2,1)S(1)}, bf16[64,4,3,256]{3,0,2,1:T(8,128)(2,1)}, u32[]{:S(2)}, u32[]{:S(2)}) collective-permute-start(bf16[64,4,3,256]{3,0,2,1:T(8,128)(2,1)S(1)} %collective-permute-done.14), channel_id=1, source_target_pairs={{4,8},{8,12},{5,9},{9,13},{6,10},{10,14},{7,11},{11,15},{20,24},{2... | collective-permute-start | bytes 1179656 | tf_op jit(solution)/shard_map/ppermute | solution.py:32
  178.3 40.3 %collective-permute-start.21 = (bf16[64,4,3,256]{3,0,2,1:T(8,128)(2,1)}, bf16[64,4,3,256]{3,0,2,1:T(8,128)(2,1)}, u32[]{:S(2)}, u32[]{:S(2)}) collective-permute-start(bf16[64,4,3,256]{3,0,2,1:T(8,128)(2,1)} %collective-permute-done.20), channel_id=1, source_target_pairs={{4,8},{8,12},{5,9},{9,13},{6,10},{10,14},{7,11},{11,15},{20,24},{2... | collective-permute-start | bytes 1179656 | tf_op jit(solution)/shard_map/ppermute | solution.py:32
  195.5 34.6 %collective-permute-start.24 = (bf16[64,4,3,256]{3,0,2,1:T(8,128)(2,1)}, bf16[64,4,3,256]{3,0,2,1:T(8,128)(2,1)}, u32[]{:S(2)}, u32[]{:S(2)}) collective-permute-start(bf16[64,4,3,256]{3,0,2,1:T(8,128)(2,1)} %collective-permute-done.23), channel_id=1, source_target_pairs={{4,0},{8,4},{5,1},{9,5},{6,2},{10,6},{7,3},{11,7},{20,16},{24,20},... | collective-permute-start | bytes 1179656 | tf_op jit(solution)/shard_map/ppermute | solution.py:33
  196.8 35.0 %collective-permute-start.16 = (bf16[64,4,3,256]{3,0,2,1:T(8,128)(2,1)}, bf16[64,4,3,256]{3,0,2,1:T(8,128)(2,1)}, u32[]{:S(2)}, u32[]{:S(2)}) collective-permute-start(bf16[64,4,3,256]{3,0,2,1:T(8,128)(2,1)} %collective-permute-done.15), channel_id=1, source_target_pairs={{8,12},{9,13},{10,14},{11,15},{24,28},{25,29},{26,30},{27,31}} | collective-permute-start | bytes 1179656 | tf_op jit(solution)/shard_map/ppermute | solution.py:32
  217.4 131.6 %reduce-scatter.15.cloned.1.call-start = ((), (), s32[]{:S(2)}) async-start(), calls=%async_computation.14 | async-start | bytes 1966080 | tf_op jit(solution)/shard_map/reduce_scatter | solution.py:63
  218.7 31.7 %collective-permute-start.22 = (bf16[64,4,3,256]{3,0,2,1:T(8,128)(2,1)}, bf16[64,4,3,256]{3,0,2,1:T(8,128)(2,1)}, u32[]{:S(2)}, u32[]{:S(2)}) collective-permute-start(bf16[64,4,3,256]{3,0,2,1:T(8,128)(2,1)} %collective-permute-done.21), channel_id=1, source_target_pairs={{8,12},{9,13},{10,14},{11,15},{24,28},{25,29},{26,30},{27,31}} | collective-permute-start | bytes 1179656 | tf_op jit(solution)/shard_map/ppermute | solution.py:32
  280.4 131.9 %reduce-scatter.17.cloned.1.call-start = ((), (), s32[]{:S(2)}) async-start(), calls=%async_computation.15 | async-start | bytes 1966080 | tf_op jit(solution)/shard_map/reduce_scatter | solution.py:63
  288.2 41.0 %collective-permute-start.35 = (bf16[64,4,3,256]{3,0,2,1:T(8,128)(2,1)S(1)}, bf16[64,4,3,256]{3,0,2,1:T(8,128)(2,1)}, u32[]{:S(2)}, u32[]{:S(2)}) collective-permute-start(bf16[64,4,3,256]{3,0,2,1:T(8,128)(2,1)S(1)} %copy.516), channel_id=1, source_target_pairs={{4,0},{8,4},{12,8},{5,1},{9,5},{13,9},{6,2},{10,6},{14,10},{7,3},{... | collective-permute-start | bytes 1179656 | tf_op jit(solution)/shard_map/ppermute | solution.py:33
  313.8 38.6 %collective-permute-start.33 = (bf16[64,4,3,256]{3,0,2,1:T(8,128)(2,1)S(1)}, bf16[64,4,3,256]{3,0,2,1:T(8,128)(2,1)}, u32[]{:S(2)}, u32[]{:S(2)}) collective-permute-start(bf16[64,4,3,256]{3,0,2,1:T(8,128)(2,1)S(1)} %collective-permute-done.32), channel_id=1, source_target_pairs={{4,8},{8,12},{5,9},{9,13},{6,10},{10,14},{7,11},{11,15},{20,24},{2... | collective-permute-start | bytes 1179656 | tf_op jit(solution)/shard_map/ppermute | solution.py:32
  329.2 34.6 %collective-permute-start.36 = (bf16[64,4,3,256]{3,0,2,1:T(8,128)(2,1)}, bf16[64,4,3,256]{3,0,2,1:T(8,128)(2,1)}, u32[]{:S(2)}, u32[]{:S(2)}) collective-permute-start(bf16[64,4,3,256]{3,0,2,1:T(8,128)(2,1)} %collective-permute-done.35), channel_id=1, source_target_pairs={{4,0},{8,4},{5,1},{9,5},{6,2},{10,6},{7,3},{11,7},{20,16},{24,20},... | collective-permute-start | bytes 1179656 | tf_op jit(solution)/shard_map/ppermute | solution.py:33
  330.6 34.7 %collective-permute-start.28 = (bf16[64,4,3,256]{3,0,2,1:T(8,128)(2,1)}, bf16[64,4,3,256]{3,0,2,1:T(8,128)(2,1)}, u32[]{:S(2)}, u32[]{:S(2)}) collective-permute-start(bf16[64,4,3,256]{3,0,2,1:T(8,128)(2,1)} %collective-permute-done.27), channel_id=1, source_target_pairs={{8,12},{9,13},{10,14},{11,15},{24,28},{25,29},{26,30},{27,31}} | collective-permute-start | bytes 1179656 | tf_op jit(solution)/shard_map/ppermute | solution.py:32
  351.0 164.4 %reduce-scatter.19.cloned.1.call-start = ((), (), s32[]{:S(2)}) async-start(), calls=%async_computation.16 | async-start | bytes 1966080 | tf_op jit(solution)/shard_map/reduce_scatter | solution.py:63
  414.3 140.4 %reduce-scatter.21.cloned.1.call-start = ((), (), s32[]{:S(2)}) async-start(), calls=%async_computation.17 | async-start | bytes 1966080 | tf_op jit(solution)/shard_map/reduce_scatter | solution.py:63
  423.3 40.1 %collective-permute-start.47 = (bf16[64,4,3,256]{3,0,2,1:T(8,128)(2,1)}, bf16[64,4,3,256]{3,0,2,1:T(8,128)(2,1)}, u32[]{:S(2)}, u32[]{:S(2)}) collective-permute-start(bf16[64,4,3,256]{3,0,2,1:T(8,128)(2,1)} %copy.518), channel_id=1, source_target_pairs={{4,0},{8,4},{12,8},{5,1},{9,5},{13,9},{6,2},{10,6},{14,10},{7,3},{... | collective-permute-start | bytes 1179656 | tf_op jit(solution)/shard_map/ppermute | solution.py:33
  432.3 32.3 %collective-permute-start.39 = (bf16[64,4,3,256]{3,0,2,1:T(8,128)(2,1)}, bf16[64,4,3,256]{3,0,2,1:T(8,128)(2,1)}, u32[]{:S(2)}, u32[]{:S(2)}) collective-permute-start(bf16[64,4,3,256]{3,0,2,1:T(8,128)(2,1)} %collective-permute-done.38), channel_id=1, source_target_pairs={{4,8},{8,12},{5,9},{9,13},{6,10},{10,14},{7,11},{11,15},{20,24},{2... | collective-permute-start | bytes 1179656 | tf_op jit(solution)/shard_map/ppermute | solution.py:32
  486.1 40.7 %collective-permute-start.49 = (bf16[64,4,3,256]{3,0,2,1:T(8,128)(2,1)}, bf16[64,4,3,256]{3,0,2,1:T(8,128)(2,1)}, u32[]{:S(2)}, u32[]{:S(2)}) collective-permute-start(bf16[64,4,3,256]{3,0,2,1:T(8,128)(2,1)} %collective-permute-done.48), channel_id=1, source_target_pairs={{4,0},{5,1},{6,2},{7,3},{20,16},{21,17},{22,18},{23,19}} | collective-permute-start | bytes 1179656 | tf_op jit(solution)/shard_map/ppermute | solution.py:33
  517.4 72.5 %all-reduce.5.cloned.1.call-start = ((), (), s32[]{:S(2)}) async-start(), calls=%async_computation.11 | async-start | bytes 131072 | tf_op jit(solution)/shard_map/psum | solution.py:168
  548.7 80.5 %reduce-scatter.23.cloned.1.call-start = ((), (), s32[]{:S(2)}) async-start(), calls=%async_computation.18 | async-start | bytes 1966080 | tf_op jit(solution)/shard_map/reduce_scatter | solution.py:63
  556.8 91.8 %reduce-scatter.27.cloned.1.call-start = ((), (), s32[]{:S(2)}) async-start(), calls=%async_computation.20 | async-start | bytes 655360 | tf_op jit(solution)/shard_map/reduce_scatter | solution.py:63
  592.6 84.0 %reduce-scatter.29.cloned.1.call-start = ((), (), s32[]{:S(2)}) async-start(), calls=%async_computation.21 | async-start | bytes 1310720 | tf_op jit(solution)/shard_map/reduce_scatter | solution.py:63
  595.6 117.1 %reduce-scatter.25.cloned.1.call-start = ((), (), s32[]{:S(2)}) async-start(), calls=%async_computation.19 | async-start | bytes 1966080 | tf_op jit(solution)/shard_map/reduce_scatter | solution.py:63
  (96 other events, 1825.5 us)
Sparse Core Ops, SparseCore 0:
  24.5 32.9 all-reduce.2
  140.3 54.0 reduce-scatter.10
  217.5 42.9 reduce-scatter.12
  280.5 44.9 reduce-scatter.14
  351.1 43.2 reduce-scatter.16
  414.4 44.7 reduce-scatter.18
  517.5 37.1 reduce-scatter.20
  557.6 30.3 all-reduce.4
  590.3 35.4 reduce-scatter.22
  627.9 20.6 reduce-scatter.26
  650.9 25.6 reduce-scatter.28
  678.7 33.9 reduce-scatter.24

commit v2 on v0

--- a/solution.py
+++ b/solution.py
@@ -17,6 +17,33 @@
         if high != low and high < count:
             route += [(low, high), (high, low)]
     return lax.ppermute(block, axis, route)
+
+
+def shared_gather(block):
+    group_count = lax.axis_size("groups")
+    dp_count = lax.axis_size("dp")
+    rows = block.shape[0]
+    if group_count == 1 or rows % group_count:
+        return lax.all_gather(block, "dp", axis=0, tiled=True)
+    share = rows // group_count
+    mine = lax.dynamic_slice_in_dim(block, lax.axis_index("groups") * share, share, axis=0)
+    gathered = lax.all_gather(mine, ("groups", "dp"), axis=0, tiled=True)
+    rest = block.shape[1:]
+    gathered = gathered.reshape((group_count, dp_count, share) + rest)
+    gathered = jnp.swapaxes(gathered, 0, 1)
+    return gathered.reshape((dp_count * rows,) + rest)
+
+
+def butterfly_sum(values, axis):
+    count = lax.axis_size(axis)
+    if count & (count - 1):
+        return lax.psum(values.astype(jnp.bfloat16), axis).astype(jnp.float32)
+    total = values
+    distance = 0
+    while (1 << distance) < count:
+        total = total + swapped(total, axis, distance)
+        distance += 1
+    return total
 
 
 def gelu_pair(values):
@@ -47,10 +74,7 @@
     blocks_here = width_here // block_size
     dp_size = lax.axis_size("dp")
     inv_root = 1.0 / math.sqrt(tokens_here * dp_size)
-    up_full, down_full = (
-        lax.all_gather(up_blocks, "dp", axis=0, tiled=True),
-        lax.all_gather(down_blocks, "dp", axis=0, tiled=True),
-    )
+    up_full, down_full = (shared_gather(up_blocks), shared_gather(down_blocks))
     sources = [inputs] + [
         swapped(inputs, "tensor", level_bit) for level_bit in range(section_count - 1)
     ]
@@ -59,7 +83,7 @@
     low_part = lax.dot_general(
         inputs, low_left, (((1,), (1,)), ((), ())), preferred_element_type=jnp.float32
     )
-    low_sum = lax.psum(low_part.astype(jnp.bfloat16), "tensor")
+    low_sum = butterfly_sum(low_part, "tensor").astype(jnp.bfloat16)
     preact = sparse.reshape(tokens_here, -1) + jnp.dot(
         low_sum, low_right, preferred_element_type=jnp.float32
     )
@@ -90,7 +114,7 @@
     back_part = lax.dot_general(
         grad_pre, low_right, (((1,), (1,)), ((), ())), preferred_element_type=jnp.float32
     )
-    back_low = lax.psum(back_part.astype(jnp.bfloat16), "tensor")
+    back_low = butterfly_sum(back_part, "tensor").astype(jnp.bfloat16)
     grad_input = (
         own_term + jnp.dot(back_low, low_left, preferred_element_type=jnp.float32)
     ).astype(jnp.bfloat16)

time: 592 us -> 543 us (0.917)
  waiting for transfers between devices: 428 us -> 344 us
  local copies, waits for them, and re-layouts: 63.8 us -> 97.6 us
    reduce_scatter x1, waiting for transfers between devices: 110 us -> 61.7 us  [shards(): lax.psum_scatter((jnp.einsum('thj,thso->jhso', row_part, picked, preferre...]
    all_gather x2, waiting for transfers between devices: 183 us -> 148 us  [shared_gather(): gathered = lax.all_gather(mine, ('groups', 'dp'), axis=0, tiled=True)]
    psum x2 -> x0, waiting for transfers between devices: 29.5 us -> none  [the longest x1 29.5 us: shards(): back_low = lax.psum(back_part.astype(jnp.bfloat16), 'tensor')]
    transpose x0 -> x4, local copies, waits for them, and re-layouts: none -> 19.6 us  [the longest x3 13.7 us: section_term(): jnp.einsum('thj,ihj->thi', grad_blocks, up_full[:, :, which_section, :],...]
    reduce_scatter x1, waiting for transfers between devices: 90.7 us -> 110 us  [shards(): lax.psum_scatter((jnp.einsum('thsi,thj->ihsj', row_part, grad_blocks, pre...]
    ppermute x4 -> x8, waiting for transfers between devices: 14.8 us -> 24.4 us  [swapped(): return lax.ppermute(block, axis, route)]
    unnamed x41 -> x53, local copies, waits for them, and re-layouts: 17.2 us -> 16.7 us
  transfers between devices with their start and end apart: 12 -> 14, of which waited for: 7 -> 8; matrix products, arithmetic and copies ran while one was open for 21% -> 23% of each run, Pallas kernels for 0% -> 0%
where the time goes in v2:
time: 543 us; the launch traced here: 542 us
  waiting for transfers between devices  344 us (63%)
  local copies, waits for them, and re-layouts  97.6 us (18%)
  matrix products  55.8 us (10%)
  other arithmetic  23.4 us (4%)
  between operations  14.5 us (3%)
  starting transfers between devices  6.68 us (1%)
    all_gather x2, waiting for transfers between devices, shared_gather(): gathered = lax.all_gather(mine, ('groups', 'dp'), axis=0, tiled=True)  148 us
    reduce_scatter x1, waiting for transfers between devices, shards(): lax.psum_scatter((jnp.einsum('thsi,thj->ihsj', row_part, grad_blocks, pre...  110 us
    reduce_scatter x1, waiting for transfers between devices, shards(): lax.psum_scatter((jnp.einsum('thj,thso->jhso', row_part, picked, preferre...  61.7 us
    ppermute x8, waiting for transfers between devices, swapped(): return lax.ppermute(block, axis, route)  24.4 us
    unnamed x53, local copies, waits for them, and re-layouts  16.7 us
    transpose x3, local copies, waits for them, and re-layouts, section_term(): jnp.einsum('thj,ihj->thi', grad_blocks, up_full[:, :, which_section, :],...  13.7 us
    another operation x4, other arithmetic, pick_blocks(): return jnp.stack(picked, axis=2)  12.8 us
    gather x6, local copies, waits for them, and re-layouts, pick_blocks(): picked.append(jnp.take(shaped, pattern[:, which_section], axis=1))  12.2 us
  transfers between devices with their start and end apart: 14, of which 8 were waited for; matrix products, arithmetic and copies ran while one was open for 23% of the time, Pallas kernels for 0%

profile of v2, /device:TPU:0, one launch (start us, length us, event | category | flops | bytes accessed | tf_op | source)
XLA Modules:
  0.0 541.9 jit_solution(4177197215838562593)
XLA Ops:
  13.2 3.0 collective-permute-start.1
  30.5 4.8 select_bitcast_fusion.3
  39.5 5.4 collective-permute-done.3
  52.0 4.7 select_bitcast_fusion
  56.7 54.8 %all-gather.3.cloned.1.call-done = bf16[256,16,3,256]{3,1,2,0:T(8,128)(2,1)} async-done(((bf16[32,16,3,256]{3,1,2,0:T(8,128)(2,1)}), bf16[256,16,3,256]{3,1,2,0:T(8,128)(2,1)}) %all-gather.3.cloned.1.call-update) | async-done | bytes 6291472 | tf_op jit(solution)/shard_map/all_gather | solution.py:30
  111.5 6.0 %copy.60 = bf16[4,2,32,16,3,256]{5,3,4,2,1,0:T(8,128)(2,1)} copy(bf16[4,2,32,16,3,256]{5,3,4,2,0,1:T(8,128)(2,1)} %bitcast.149) | data formatting | bytes 12582912 | tf_op jit(solution)/shard_map/transpose | solution.py:33
  117.5 93.0 %all-gather.5.cloned.1.call-done = bf16[256,16,3,256]{3,1,2,0:T(8,128)(2,1)} async-done(((bf16[32,16,3,256]{3,1,2,0:T(8,128)(2,1)}), bf16[256,16,3,256]{3,1,2,0:T(8,128)(2,1)}) %all-gather.5.cloned.1.call-update) | async-done | bytes 6291472 | tf_op jit(solution)/shard_map/all_gather | solution.py:30
  210.6 5.2 copy.62
  215.8 3.4 fusion.12
  219.1 5.6 %copy.75 = f32[256,4096]{1,0:T(8,128)} copy(f32[256,4096]{0,1:T(8,128)} %bitcast.152) | data formatting | bytes 8388608 | tf_op jit(solution)/shard_map/reshape | solution.py:95
  224.8 11.1 %fusion.2 = f32[16,256,256,1]{2,1,3,0:T(8,128)} fusion(bf16[256,16,3,256]{3,1,2,0:T(8,128)(2,1)} %bitcast.141, bf16[256,16,1,256]{3,0,2,1:T(8,128)(2,1)} %get-tuple-element.51, bf16[256,16,1,256]{3,0,2,1:T(8,128)(2,1)} %get-tuple-element.52, bf16[256,16,1,256]{3,0,2,1:T(8,128)(2,1)} %select_bitcast_fusion.2), kind=kOutput, calls=%fused_computation.12 | convolution fusion | flops 1616904192 | bytes 16777216 | tf_op jit(solution)/shard_map/thsi,ihsj->thj/dot_general | solution.py:82
  235.9 5.7 %copy.74 = f32[256,4096]{1,0:T(8,128)} copy(f32[256,4096]{0,1:T(8,128)} %bitcast.153) | data formatting | bytes 8388608 | tf_op jit(solution)/shard_map/reshape | solution.py:87
  241.7 6.7 %multiply_convert_fusion.2 = (bf16[256,4096]{1,0:T(8,128)(2,1)}, bf16[256,4096]{1,0:T(8,128)(2,1)S(1)}) fusion(f32[256,4096]{1,0:T(8,128)} %copy.75, f32[256,4096]{1,0:T(8,128)} %copy.74, bf16[256,128]{1,0:T(8,128)(2,1)S(1)} %add_convert_fusion.2, bf16[128,4096]{1,0:T(8,128)(2,1)S(1)} %copy-done.20), kind=kOutput, calls=%fused_computation.26 | convolution fusion | flops 291504128 | bytes 13697024 | tf_op jit(solution)/shard_map/dot_general | solution.py:87
  253.4 4.1 collective-permute-done.7
  258.7 3.1 fusion.4
  261.9 2.5 copy.106
  264.8 6.8 %fusion.1 = bf16[256,16,3,256]{0,3,2,1:T(8,128)(2,1)} fusion(bf16[256,16,1,256]{3,0,2,1:T(8,128)(2,1)S(1)} %copy-done.11, bf16[256,16,1,256]{3,0,2,1:T(8,128)(2,1)S(1)} %copy-done.13, bf16[256,16,1,256]{3,0,2,1:T(8,128)(2,1)} %select_bitcast_fusion.5, bf16[256,16,256,1]{2,1,0,3:T(8,128)(2,1)S(1)} %bitcast.158), kind=kOutput, calls=%fused_computation.9 | convolution fusion | flops 1623195648 | bytes 14680064 | tf_op jit(solution)/shard_map/thj,thso->jhso/dot_general | solution.py:135
  271.6 9.0 %copy.88 = bf16[256,16,3,256]{3,1,2,0:T(8,128)(2,1)} copy(bf16[256,16,3,256]{0,3,2,1:T(8,128)(2,1)} %fusion.1) | data formatting | bytes 12582912 | tf_op jit(solution)/shard_map/convert_element_type | solution.py:137
  280.8 2.4 copy.105
  283.6 6.3 %fusion = bf16[256,16,3,256]{0,3,2,1:T(8,128)(2,1)} fusion(bf16[256,16,1,256]{3,0,2,1:T(8,128)(2,1)S(1)} %copy-done.14, bf16[256,16,1,256]{3,0,2,1:T(8,128)(2,1)S(1)} %copy-done.15, bf16[256,16,1,256]{3,0,2,1:T(8,128)(2,1)} %select_bitcast_fusion.2, bf16[256,16,256,1]{2,1,0,3:T(8,128)(2,1)S(1)} %bitcast.159), kind=kOutput, calls=%fused_computation.8 | convolution fusion | flops 1635778560 | bytes 14680064 | tf_op jit(solution)/shard_map/thsi,thj->ihsj/dot_general | solution.py:124
  289.9 9.1 %copy.85 = bf16[256,16,3,256]{3,1,2,0:T(8,128)(2,1)} copy(bf16[256,16,3,256]{0,3,2,1:T(8,128)(2,1)} %fusion) | data formatting | bytes 12582912 | tf_op jit(solution)/shard_map/convert_element_type | solution.py:126
  299.0 5.5 %fusion.36 = (bf16[256,16,1,256]{3,1,2,0:T(8,128)(2,1)S(1)}, bf16[256,16,1,256]{3,1,2,0:T(8,128)(2,1)}, bf16[256,16,1,256]{3,1,2,0:T(8,128)(2,1)}) fusion(bf16[256,16,3,256]{3,1,2,0:T(8,128)(2,1)} %bitcast.142), kind=kLoop, calls=%fused_computation.92 | loop fusion | bytes 12582912 | tf_op jit(solution)/shard_map/slice | solution.py:104
  304.5 2.3 convolution_bitcast_fusion.1
  306.9 4.6 copy.80
  317.7 4.6 copy.83
  329.2 4.5 copy.77
  336.7 13.5 %collective-permute-done.5 = bf16[256,2048]{1,0:T(8,128)(2,1)S(1)} collective-permute-done((bf16[256,2048]{1,0:T(8,128)(2,1)}, bf16[256,2048]{1,0:T(8,128)(2,1)S(1)}, u32[]{:S(2)}, u32[]{:S(2)}) %collective-permute-start.5) | collective-permute-done | bytes 1048608 | tf_op jit(solution)/shard_map/ppermute | solution.py:19
  350.2 2.7 add_convert_fusion
  356.4 61.7 %reduce-scatter.7.cloned.1.call-done = bf16[64,16,3,256]{3,1,2,0:T(8,128)(2,1)} async-done(((bf16[256,16,3,256]{3,1,2,0:T(8,128)(2,1)}), bf16[64,16,3,256]{3,1,2,0:T(8,128)(2,1)}) %reduce-scatter.7.cloned.1.call-update) | async-done | bytes 1572880 | tf_op jit(solution)/shard_map/reduce_scatter | solution.py:133
  418.0 3.6 convert_element_type.90
  421.7 109.9 %reduce-scatter.5.cloned.1.call-done = bf16[64,16,3,256]{3,1,2,0:T(8,128)(2,1)} async-done(((bf16[256,16,3,256]{3,1,2,0:T(8,128)(2,1)}), bf16[64,16,3,256]{3,1,2,0:T(8,128)(2,1)}) %reduce-scatter.5.cloned.1.call-update) | async-done | bytes 1572880 | tf_op jit(solution)/shard_map/reduce_scatter | solution.py:122
  531.5 3.5 convert_element_type.86
  (114 shorter events, 58.2 us)
Async XLA Ops:
  7.2 104.4 %all-gather.3.cloned.1.call-start = ((), (), s32[]{:S(2)}) async-start(), calls=%async_computation.4 | async-start | bytes 7077888 | tf_op jit(solution)/shard_map/all_gather | solution.py:30
  8.6 3.2 copy-start.6
  9.5 6.6 %copy-start.16 = (bf16[128,2048]{1,0:T(8,128)(2,1)S(1)}, bf16[128,2048]{1,0:T(8,128)(2,1)}, u32[]{:S(2)}) copy-start(bf16[128,2048]{1,0:T(8,128)(2,1)} %param.14) | copy-start | bytes 1572868
  9.6 201.0 %all-gather.5.cloned.1.call-start = ((), (), s32[]{:S(2)}) async-start(), calls=%async_computation.5 | async-start | bytes 7077888 | tf_op jit(solution)/shard_map/all_gather | solution.py:30
  11.7 341.2 %reduce-scatter.9.cloned.1.call-start = ((), (), s32[]{:S(2)}) async-start(), calls=%async_computation.8 | async-start | bytes 655360 | tf_op jit(solution)/shard_map/reduce_scatter | solution.py:143
  13.2 31.7 %collective-permute-start.1 = (bf16[256,2048]{0,1:T(8,128)(2,1)}, bf16[256,2048]{0,1:T(8,128)(2,1)}, u32[]{:S(2)}, u32[]{:S(2)}) collective-permute-start(bf16[256,2048]{0,1:T(8,128)(2,1)} %copy.67), channel_id=1, source_target_pairs={{0,2},{2,0},{1,3},{3,1},{4,6},{6,4},{5,7},{7,5},{8,10},{10,8},{9,1... | collective-permute-start | bytes 3145736 | tf_op jit(solution)/shard_map/ppermute | solution.py:19
  16.1 30.2 %collective-permute-start = (bf16[256,2048]{0,1:T(8,128)(2,1)}, bf16[256,2048]{0,1:T(8,128)(2,1)}, u32[]{:S(2)}, u32[]{:S(2)}) collective-permute-start(bf16[256,2048]{0,1:T(8,128)(2,1)} %copy.67), channel_id=1, source_target_pairs={{0,1},{1,0},{2,3},{3,2},{4,5},{5,4},{6,7},{7,6},{8,9},{9,8},{10,11... | collective-permute-start | bytes 3145736 | tf_op jit(solution)/shard_map/ppermute | solution.py:19
  16.6 22.8 %collective-permute-start.2 = (f32[256,128]{1,0:T(8,128)S(1)}, f32[256,128]{1,0:T(8,128)S(1)}, u32[]{:S(2)}, u32[]{:S(2)}) collective-permute-start(f32[256,128]{1,0:T(8,128)S(1)} %fusion.37), channel_id=1, source_target_pairs={{0,1},{1,0},{2,3},{3,2},{4,5},{5,4},{6,7},{7,6},{8,9},{9,8},{10,11... | collective-permute-start | bytes 393224 | tf_op jit(solution)/shard_map/ppermute | solution.py:19
  18.6 3.8 copy-start.22
  30.5 4.8 copy-start.9
  39.3 5.5 %collective-permute-start.3 = (f32[256,128]{1,0:T(8,128)S(1)}, f32[256,128]{1,0:T(8,128)S(1)}, u32[]{:S(2)}, u32[]{:S(2)}) collective-permute-start(f32[256,128]{1,0:T(8,128)S(1)} %add.53), channel_id=1, source_target_pairs={{0,2},{2,0},{1,3},{3,1},{4,6},{6,4},{5,7},{7,5},{8,10},{10,8},{9,1... | collective-permute-start | bytes 393224 | tf_op jit(solution)/shard_map/ppermute | solution.py:19
  210.6 5.2 copy-start.10
  210.6 5.2 copy-start.12
  210.6 5.2 copy-start.17
  235.9 5.7 %copy-start.20 = (bf16[128,4096]{1,0:T(8,128)(2,1)S(1)}, bf16[128,4096]{1,0:T(8,128)(2,1)}, u32[]{:S(2)}) copy-start(bf16[128,4096]{1,0:T(8,128)(2,1)} %param.15) | copy-start | bytes 3145732
  248.4 9.2 %copy-start.7 = (bf16[256,2048]{1,0:T(8,128)(2,1)S(1)}, bf16[256,2048]{1,0:T(8,128)(2,1)}, u32[]{:S(2)}) copy-start(bf16[256,2048]{1,0:T(8,128)(2,1)} %param.10) | copy-start | bytes 3145732
  250.4 1.4 collective-permute-start.6
  251.9 5.6 %collective-permute-start.7 = (f32[256,128]{1,0:T(8,128)S(1)}, f32[256,128]{1,0:T(8,128)S(1)}, u32[]{:S(2)}, u32[]{:S(2)}) collective-permute-start(f32[256,128]{1,0:T(8,128)S(1)} %add.62), channel_id=1, source_target_pairs={{0,2},{2,0},{1,3},{3,1},{4,6},{6,4},{5,7},{7,5},{8,10},{10,8},{9,1... | collective-permute-start | bytes 393224 | tf_op jit(solution)/shard_map/ppermute | solution.py:19
  258.7 95.9 %reduce-scatter.11.cloned.1.call-start = ((), (), s32[]{:S(2)}) async-start(), calls=%async_computation.9 | async-start | bytes 1310720 | tf_op jit(solution)/shard_map/reduce_scatter | solution.py:155
  261.8 156.2 %reduce-scatter.7.cloned.1.call-start = ((), (), s32[]{:S(2)}) async-start(), calls=%async_computation.7 | async-start | bytes 7864320 | tf_op jit(solution)/shard_map/reduce_scatter | solution.py:133
  261.9 2.5 copy-start.11
  261.9 3.0 copy-start.13
  280.7 250.8 %reduce-scatter.5.cloned.1.call-start = ((), (), s32[]{:S(2)}) async-start(), calls=%async_computation.6 | async-start | bytes 7864320 | tf_op jit(solution)/shard_map/reduce_scatter | solution.py:122
  280.8 2.8 copy-start.15
  299.0 5.5 %copy-start.3 = (bf16[256,4096]{1,0:T(8,128)(2,1)S(1)}, bf16[256,4096]{1,0:T(8,128)(2,1)}, u32[]{:S(2)}) copy-start(bf16[256,4096]{1,0:T(8,128)(2,1)} %copy-done.2) | copy-start | bytes 6291460
  311.4 2.7 copy-start.4
  311.4 4.0 copy-start.19
  314.0 22.7 %collective-permute-start.4 = (bf16[256,2048]{1,0:T(8,128)(2,1)S(1)}, bf16[256,2048]{1,0:T(8,128)(2,1)}, u32[]{:S(2)}, u32[]{:S(2)}) collective-permute-start(bf16[256,2048]{1,0:T(8,128)(2,1)S(1)} %bitcast.160), channel_id=1, source_target_pairs={{0,1},{1,0},{2,3},{3,2},{4,5},{5,4},{6,7},{7,6},{8,9},{9,8},{10,11... | collective-permute-start | bytes 3145736 | tf_op jit(solution)/shard_map/ppermute | solution.py:19
  322.3 4.6 copy-start.5
  322.3 4.6 copy-start.18
  325.8 24.4 %collective-permute-start.5 = (bf16[256,2048]{1,0:T(8,128)(2,1)}, bf16[256,2048]{1,0:T(8,128)(2,1)S(1)}, u32[]{:S(2)}, u32[]{:S(2)}) collective-permute-start(bf16[256,2048]{1,0:T(8,128)(2,1)} %bitcast.71), channel_id=1, source_target_pairs={{0,2},{2,0},{1,3},{3,1},{4,6},{6,4},{5,7},{7,5},{8,10},{10,8},{9,1... | collective-permute-start | bytes 3145736 | tf_op jit(solution)/shard_map/ppermute | solution.py:19
  418.0 117.0 %copy-start.1 = (bf16[64,16,3,256]{3,1,2,0:T(8,128)(2,1)S(1)}, bf16[64,16,3,256]{3,1,2,0:T(8,128)(2,1)}, u32[]{:S(2)}) copy-start(bf16[64,16,3,256]{3,1,2,0:T(8,128)(2,1)} %param.12) | copy-start | bytes 4718596
  (5 other events, 9.6 us)
Sparse Core Ops, SparseCore 0:
  10.1 101.4 all-gather.2
  113.6 96.8 all-gather.4
  258.8 20.0 reduce-scatter.8
  281.0 25.5 reduce-scatter.10
  308.7 109.2 reduce-scatter.6
  420.2 111.2 reduce-scatter.4

commit v3 on v2

--- a/solution.py
+++ b/solution.py
@@ -19,7 +19,7 @@
     return lax.ppermute(block, axis, route)
 
 
-def shared_gather(block):
+def shared_gather(block, after=None):
     group_count = lax.axis_size("groups")
     dp_count = lax.axis_size("dp")
     rows = block.shape[0]
@@ -27,11 +27,42 @@
         return lax.all_gather(block, "dp", axis=0, tiled=True)
     share = rows // group_count
     mine = lax.dynamic_slice_in_dim(block, lax.axis_index("groups") * share, share, axis=0)
-    gathered = lax.all_gather(mine, ("groups", "dp"), axis=0, tiled=True)
-    rest = block.shape[1:]
-    gathered = gathered.reshape((group_count, dp_count, share) + rest)
-    gathered = jnp.swapaxes(gathered, 0, 1)
-    return gathered.reshape((dp_count * rows,) + rest)
+    if after is not None:
+        mine, _ = lax.optimization_barrier((mine, after))
+    return lax.all_gather(mine, ("dp", "groups"), axis=0, tiled=True)
+
+
+def line_scatter(parts, axis):
+    count = lax.axis_size(axis)
+    if count > 8:
+        return lax.psum_scatter(parts, axis, scatter_dimension=0, tiled=False).astype(jnp.float32)
+    me = lax.axis_index(axis)
+    own = lax.dynamic_index_in_dim(parts, me, 0, keepdims=False).astype(jnp.float32)
+    if count == 1:
+        return own
+    rightward = leftward = None
+    for step in range(1, count):
+        ahead = lax.dynamic_index_in_dim(
+            parts, jnp.clip(me + count - step, 0, count - 1), 0, keepdims=False
+        ).astype(jnp.float32)
+        behind = lax.dynamic_index_in_dim(
+            parts, jnp.clip(me - count + step, 0, count - 1), 0, keepdims=False
+        ).astype(jnp.float32)
+        if rightward is not None:
+            ahead = ahead + rightward.astype(jnp.float32)
+            behind = behind + leftward.astype(jnp.float32)
+        rightward = lax.ppermute(
+            ahead.astype(jnp.bfloat16), axis, [(i, i + 1) for i in range(0, min(step, count - 1))]
+        )
+        leftward = lax.ppermute(
+            behind.astype(jnp.bfloat16), axis, [(i, i - 1) for i in range(max(count - step, 1), count)]
+        )
+    return own + rightward.astype(jnp.float32) + leftward.astype(jnp.float32)
+
+
+def split_rows(values, axis, count):
+    rows = values.shape[axis] // count
+    return [lax.slice_in_dim(values, d * rows, (d + 1) * rows, axis=axis) for d in range(count)]
 
 
 def butterfly_sum(values, axis):
@@ -74,7 +105,7 @@
     blocks_here = width_here // block_size
     dp_size = lax.axis_size("dp")
     inv_root = 1.0 / math.sqrt(tokens_here * dp_size)
-    up_full, down_full = (shared_gather(up_blocks), shared_gather(down_blocks))
+    up_full = shared_gather(up_blocks)
     sources = [inputs] + [
         swapped(inputs, "tensor", level_bit) for level_bit in range(section_count - 1)
     ]
@@ -90,11 +121,42 @@
     activated, slopes = gelu_pair(preact)
     hidden = activated.astype(jnp.bfloat16)
     picked = pick_blocks([cotangent] * section_count, down_pattern, block_size)
+    down_full = shared_gather(down_blocks, hidden)
+    hidden_blocks = hidden.reshape(tokens_here, hidden_here, block_size)
+    grad_down = line_scatter(
+        (
+            jnp.stack(
+                [
+                    jnp.einsum("thj,thso->hjso", rows, picked, preferred_element_type=jnp.float32)
+                    for rows in split_rows(hidden_blocks, 2, dp_size)
+                ]
+            )
+            * inv_root
+        ).astype(jnp.bfloat16),
+        "dp",
+    )
+    grad_down = jnp.transpose(grad_down, (1, 0, 2, 3))
+    down_full, grad_down = lax.optimization_barrier((down_full, grad_down))
     grad_hidden = jnp.einsum(
         "thso,jhso->thj", picked, down_full, preferred_element_type=jnp.float32
     ).reshape(tokens_here, -1)
     grad_pre = (grad_hidden * slopes).astype(jnp.bfloat16)
     grad_blocks = grad_pre.reshape(tokens_here, hidden_here, block_size)
+    grad_up = lax.psum_scatter(
+        (
+            jnp.stack(
+                [
+                    jnp.einsum("thsi,thj->hsij", rows, grad_blocks, preferred_element_type=jnp.float32)
+                    for rows in split_rows(selected, 3, dp_size)
+                ]
+            )
+            * inv_root
+        ).astype(jnp.bfloat16),
+        "dp",
+        scatter_dimension=0,
+        tiled=False,
+    ).astype(jnp.float32)
+    grad_up = jnp.transpose(grad_up, (2, 0, 1, 3))
     slot_ids = jnp.arange(blocks_here, dtype=jnp.int32)
 
     def section_term(which_section):
@@ -118,40 +180,19 @@
     grad_input = (
         own_term + jnp.dot(back_low, low_left, preferred_element_type=jnp.float32)
     ).astype(jnp.bfloat16)
-    row_part = selected
-    grad_up = lax.psum_scatter(
-        (
-            jnp.einsum("thsi,thj->ihsj", row_part, grad_blocks, preferred_element_type=jnp.float32)
+    row_part, low_row_part, grad_up = lax.optimization_barrier((back_low, low_sum, grad_up))
+    grad_left = lax.psum_scatter(
+        (
+            lax.dot_general(
+                row_part, inputs, (((0,), (0,)), ((), ())), preferred_element_type=jnp.float32
+            )
             * inv_root
         ).astype(jnp.bfloat16),
         "dp",
         scatter_dimension=0,
         tiled=True,
     ).astype(jnp.float32)
-    hidden_blocks = hidden.reshape(tokens_here, hidden_here, block_size)
-    row_part = hidden_blocks
-    grad_down = lax.psum_scatter(
-        (
-            jnp.einsum("thj,thso->jhso", row_part, picked, preferred_element_type=jnp.float32)
-            * inv_root
-        ).astype(jnp.bfloat16),
-        "dp",
-        scatter_dimension=0,
-        tiled=True,
-    ).astype(jnp.float32)
-    row_part = back_low
-    grad_left = lax.psum_scatter(
-        (
-            lax.dot_general(
-                row_part, inputs, (((0,), (0,)), ((), ())), preferred_element_type=jnp.float32
-            )
-            * inv_root
-        ).astype(jnp.bfloat16),
-        "dp",
-        scatter_dimension=0,
-        tiled=True,
-    ).astype(jnp.float32)
-    row_part = low_sum
+    row_part = low_row_part
     grad_right = lax.psum_scatter(
         (
             lax.dot_general(

time: 543 us -> 599 us (1.10); the launches traced: 542 us -> 590 us
  other arithmetic: 23.4 us -> 54.8 us
  local copies, waits for them, and re-layouts: 97.6 us -> 68.1 us
  starting transfers between devices: 6.68 us -> 26.6 us
  waiting for transfers between devices: 344 us -> 362 us
  matrix products: 55.8 us -> 63.8 us
    ppermute x0 -> x6, waiting for transfers between devices: none -> 172 us  [the longest x3 132 us: line_scatter(): lax.ppermute(ahead.astype(jnp.bfloat16), axis, [(i, i + 1) for i in range...]
    all_gather x2, waiting for transfers between devices: 148 us -> 59.6 us  [shared_gather(): return lax.all_gather(mine, ('dp', 'groups'), axis=0, tiled=True)]
    reduce_scatter x2 -> x1, waiting for transfers between devices: 172 us -> 101 us  [shards(): lax.psum_scatter((jnp.stack([jnp.einsum('thsi,thj->hsij', rows, grad_bloc...]
    ppermute x0 -> x6, starting transfers between devices: none -> 19.1 us  [the longest x3 14 us: line_scatter(): lax.ppermute(ahead.astype(jnp.bfloat16), axis, [(i, i + 1) for i in range...]
    convert_element_type x2 -> x0, local copies, waits for them, and re-layouts: 18.1 us -> none  [the longest x1 9.06 us: shards(): grad_up = lax.psum_scatter((jnp.einsum('thsi,thj->ihsj', row_part, grad_b...]
    convert_element_type x2 -> x6, other arithmetic: 7.16 us -> 24.5 us  [the longest x2 9.76 us: line_scatter(): ahead.astype(jnp.bfloat16)]
    transpose x0 -> x2, other arithmetic: none -> 8.34 us  [the longest x1 4.87 us: shards(): grad_down = jnp.transpose(grad_down, (1, 0, 2, 3))]
    unnamed x53 -> x55, local copies, waits for them, and re-layouts: 16.7 us -> 22.9 us
  transfers between devices with their start and end apart: 14 -> 19, of which waited for: 8 -> 10; matrix products, arithmetic and copies ran while one was open for 23% -> 20% of each run, Pallas kernels for 0% -> 0%
where the time goes in v3:
time: 599 us; the launch traced here: 590 us
  waiting for transfers between devices  362 us (60%)
  local copies, waits for them, and re-layouts  68.1 us (11%)
  matrix products  63.8 us (11%)
  other arithmetic  54.8 us (9%)
  starting transfers between devices  26.6 us (4%)
  between operations  14.7 us (2%)
    ppermute x3, waiting for transfers between devices, line_scatter(): lax.ppermute(ahead.astype(jnp.bfloat16), axis, [(i, i + 1) for i in range...  132 us
    reduce_scatter x1, waiting for transfers between devices, shards(): lax.psum_scatter((jnp.stack([jnp.einsum('thsi,thj->hsij', rows, grad_bloc...  101 us
    all_gather x2, waiting for transfers between devices, shared_gather(): return lax.all_gather(mine, ('dp', 'groups'), axis=0, tiled=True)  59.6 us
    ppermute x3, waiting for transfers between devices, line_scatter(): lax.ppermute(behind.astype(jnp.bfloat16), axis, [(i, i - 1) for i in rang...  40 us
    ppermute x8, waiting for transfers between devices, swapped(): return lax.ppermute(block, axis, route)  29.6 us
    unnamed x55, local copies, waits for them, and re-layouts  22.9 us
    another operation x5, other arithmetic, pick_blocks(): return jnp.stack(picked, axis=2)  18.4 us
    ppermute x3, starting transfers between devices, line_scatter(): lax.ppermute(ahead.astype(jnp.bfloat16), axis, [(i, i + 1) for i in range...  14 us
  transfers between devices with their start and end apart: 19, of which 10 were waited for; matrix products, arithmetic and copies ran while one was open for 20% of the time, Pallas kernels for 0%

profile of v3, /device:TPU:0, one launch (start us, length us, event | category | flops | bytes accessed | tf_op | source)
XLA Modules:
  0.0 589.8 jit_solution(18238871453490536873)
XLA Ops:
  22.5 4.1 select_bitcast_fusion
  28.1 12.9 %collective-permute-done.3 = f32[256,128]{1,0:T(8,128)S(1)} collective-permute-done((f32[256,128]{1,0:T(8,128)S(1)}, f32[256,128]{1,0:T(8,128)S(1)}, u32[]{:S(2)}, u32[]{:S(2)}) %collective-permute-start.3) | collective-permute-done | bytes 131104 | tf_op jit(solution)/shard_map/ppermute | solution.py:19
  48.1 4.0 select_bitcast_fusion.3
  52.1 59.6 %all-gather.3.cloned.1.call-done = bf16[256,16,3,256]{3,0,2,1:T(8,128)(2,1)} async-done(((bf16[32,16,3,256]{3,0,2,1:T(8,128)(2,1)}), bf16[256,16,3,256]{3,0,2,1:T(8,128)(2,1)}) %all-gather.3.cloned.1.call-update) | async-done | bytes 6291472 | tf_op jit(solution)/shard_map/all_gather | solution.py:32
  111.7 8.3 %fusion.59 = f32[16,256,256,1]{2,1,3,0:T(8,128)} fusion(bf16[256,16,3,256]{3,0,2,1:T(8,128)(2,1)} %all-gather.3.cloned.1.call-done, bf16[256,16,1,256]{3,0,2,1:T(8,128)(2,1)S(1)} %get-tuple-element.67, bf16[256,16,1,256]{3,0,2,1:T(8,128)(2,1)} %get-tuple-element.68, bf16[256,16,1,256]{3,0,2,1:T(8,128)(2,1)} %select_bitcast_fusion.5), kind=kOutput, calls=%fused_computation.123 | convolution fusion | flops 1616904192 | bytes 16777216 | tf_op jit(solution)/shard_map/thsi,ihsj->thj/dot_general | solution.py:113
  119.9 5.6 copy.90
  125.5 6.9 %multiply_convert_fusion = (bf16[256,4096]{1,0:T(8,128)(2,1)}, f32[256,4096]{1,0:T(8,128)}) fusion(f32[256,4096]{1,0:T(8,128)} %copy.90, bf16[256,128]{1,0:T(8,128)(2,1)S(1)} %add_convert_fusion.2, bf16[128,4096]{1,0:T(8,128)(2,1)} %param.15), kind=kOutput, calls=%fused_computation.26 | convolution fusion | flops 278921216 | bytes 11599872 | tf_op jit(solution)/shard_map/dot_general | solution.py:118
  137.7 4.2 copy.140
  141.9 3.7 convolution_bitcast_fusion.6
  164.0 57.3 %collective-permute-done.4 = bf16[16,64,3,256]{3,1,2,0:T(8,128)(2,1)} collective-permute-done((bf16[16,64,3,256]{3,1,2,0:T(8,128)(2,1)}, bf16[16,64,3,256]{3,1,2,0:T(8,128)(2,1)}, u32[]{:S(2)}, u32[]{:S(2)}) %collective-permute-start.4) | collective-permute-done | bytes 1572896 | tf_op jit(solution)/shard_map/ppermute | solution.py:54
  221.3 3.7 fusion.22
  225.0 5.6 collective-permute-start.5
  230.6 52.7 %collective-permute-done.5 = bf16[16,64,3,256]{3,1,2,0:T(8,128)(2,1)} collective-permute-done((bf16[16,64,3,256]{3,1,2,0:T(8,128)(2,1)}, bf16[16,64,3,256]{3,1,2,0:T(8,128)(2,1)}, u32[]{:S(2)}, u32[]{:S(2)}) %collective-permute-start.5) | collective-permute-done | bytes 1572896 | tf_op jit(solution)/shard_map/ppermute | solution.py:54
  283.3 6.0 %fusion.23 = (bf16[16,64,3,256]{3,1,2,0:T(8,128)(2,1)}, bf16[16,64,3,256]{3,1,2,0:T(8,128)(2,1)}) fusion(bf16[16,64,3,256]{3,1,2,0:T(8,128)(2,1)} %collective-permute-done.5, bf16[4,16,64,3,256]{4,2,3,1,0:T(8,128)(2,1)} %copy-done.2, s32[]{:T(128)S(6)} %min.19, bf16[16,64,3,256]{3,1,2,0:T(8,128)(2,1)} %collective-permute-done.7, s32[]{:T(128)S(6)} %min.23), kind=kLoop, calls=%fused_computation.43 | loop fusion | flops 6291456 | bytes 9437192 | tf_op jit(solution)/shard_map/convert_element_type | solution.py:55
  291.1 5.0 collective-permute-start.6
  296.2 3.7 fusion.21
  301.2 5.5 pad_maximum_fusion
  306.7 21.6 %collective-permute-done.6 = bf16[16,64,3,256]{3,1,2,0:T(8,128)(2,1)} collective-permute-done((bf16[16,64,3,256]{3,1,2,0:T(8,128)(2,1)}, bf16[16,64,3,256]{3,1,2,0:T(8,128)(2,1)}, u32[]{:S(2)}, u32[]{:S(2)}) %collective-permute-start.6) | collective-permute-done | bytes 1572896 | tf_op jit(solution)/shard_map/ppermute | solution.py:54
  328.3 40.0 %collective-permute-done.9 = bf16[16,64,3,256]{3,1,2,0:T(8,128)(2,1)} collective-permute-done((bf16[16,64,3,256]{3,1,2,0:T(8,128)(2,1)}, bf16[16,64,3,256]{3,1,2,0:T(8,128)(2,1)}, u32[]{:S(2)}, u32[]{:S(2)}) %collective-permute-start.9) | collective-permute-done | bytes 1572896 | tf_op jit(solution)/shard_map/ppermute | solution.py:57
  368.3 4.9 fusion.25
  373.2 8.5 %fusion.2 = f32[16,256,256,1]{2,1,3,0:T(8,128)} fusion(bf16[256,16,3,256]{3,1,2,0:T(8,128)(2,1)} %all-gather.5.cloned.1.call-done, bf16[256,16,1,256]{3,0,2,1:T(8,128)(2,1)S(1)} %copy-done.10, bf16[256,16,1,256]{3,0,2,1:T(8,128)(2,1)} %get-tuple-element.70, bf16[256,16,1,256]{3,0,2,1:T(8,128)(2,1)} %select_bitcast_fusion.2), kind=kOutput, calls=%fused_computation.12 | convolution fusion | flops 1616904192 | bytes 16777216 | tf_op jit(solution)/shard_map/thso,jhso->thj/dot_general | solution.py:140
  381.6 5.8 copy.131
  387.4 5.3 fusion.11
  403.7 3.9 fusion.1
  413.4 3.9 collective-permute-done.13
  417.3 100.9 %reduce-scatter.4.cloned.1.call-done = bf16[1,16,3,64,256]{4,3,2,1,0:T(8,128)(2,1)} async-done(((bf16[4,16,3,64,256]{4,3,2,1,0:T(8,128)(2,1)}), bf16[1,16,3,64,256]{4,3,2,1,0:T(8,128)(2,1)}) %reduce-scatter.4.cloned.1.call-update) | async-done | bytes 1572880 | tf_op jit(solution)/shard_map/reduce_scatter | solution.py:145
  523.1 3.7 convolution_bitcast_fusion.1
  526.9 4.5 copy.104
  535.3 3.8 convolution_bitcast_fusion
  539.0 4.5 copy.106
  548.4 3.7 convolution_bitcast_fusion.2
  561.3 11.5 %collective-permute-done.11 = bf16[256,2048]{1,0:T(8,128)(2,1)} collective-permute-done((bf16[256,2048]{1,0:T(8,128)(2,1)}, bf16[256,2048]{1,0:T(8,128)(2,1)}, u32[]{:S(2)}, u32[]{:S(2)}) %collective-permute-start.11) | collective-permute-done | bytes 1048608 | tf_op jit(solution)/shard_map/ppermute | solution.py:19
  (136 shorter events, 99.7 us)
Async XLA Ops:
  7.2 7.0 %copy-start.12 = (bf16[128,2048]{1,0:T(8,128)(2,1)S(1)}, bf16[128,2048]{1,0:T(8,128)(2,1)}, u32[]{:S(2)}) copy-start(bf16[128,2048]{1,0:T(8,128)(2,1)} %param.14) | copy-start | bytes 1572868
  7.2 104.5 %all-gather.3.cloned.1.call-start = ((), (), s32[]{:S(2)}) async-start(), calls=%async_computation.3 | async-start | bytes 7077888 | tf_op jit(solution)/shard_map/all_gather | solution.py:32
  9.8 6.6 %copy-start.19 = (s32[16,3]{0,1:T(4,128)S(1)}, s32[16,3]{0,1:T(4,128)}, u32[]{:S(2)}) copy-start(s32[16,3]{0,1:T(4,128)} %param.16) | copy-start | bytes 580
  9.8 363.3 %all-gather.5.cloned.1.call-start = ((), (), s32[]{:S(2)}) async-start(), calls=%async_computation.4 | async-start | bytes 7077888 | tf_op jit(solution)/shard_map/all_gather | solution.py:32
  11.2 29.8 %collective-permute-start = (bf16[256,2048]{0,1:T(8,128)(2,1)}, bf16[256,2048]{0,1:T(8,128)(2,1)}, u32[]{:S(2)}, u32[]{:S(2)}) collective-permute-start(bf16[256,2048]{0,1:T(8,128)(2,1)} %copy.84), channel_id=1, source_target_pairs={{0,1},{1,0},{2,3},{3,2},{4,5},{5,4},{6,7},{7,6},{8,9},{9,8},{10,11... | collective-permute-start | bytes 3145736 | tf_op jit(solution)/shard_map/ppermute | solution.py:19
  11.7 30.8 %collective-permute-start.1 = (bf16[256,2048]{0,1:T(8,128)(2,1)}, bf16[256,2048]{0,1:T(8,128)(2,1)}, u32[]{:S(2)}, u32[]{:S(2)}) collective-permute-start(bf16[256,2048]{0,1:T(8,128)(2,1)} %copy.84), channel_id=1, source_target_pairs={{0,2},{2,0},{1,3},{3,1},{4,6},{6,4},{5,7},{7,5},{8,10},{10,8},{9,1... | collective-permute-start | bytes 3145736 | tf_op jit(solution)/shard_map/ppermute | solution.py:19
  14.6 12.1 %collective-permute-start.2 = (f32[256,128]{1,0:T(8,128)S(1)}, f32[256,128]{1,0:T(8,128)S(1)}, u32[]{:S(2)}, u32[]{:S(2)}) collective-permute-start(f32[256,128]{1,0:T(8,128)S(1)} %fusion.60), channel_id=1, source_target_pairs={{0,1},{1,0},{2,3},{3,2},{4,5},{5,4},{6,7},{7,6},{8,9},{9,8},{10,11... | collective-permute-start | bytes 393224 | tf_op jit(solution)/shard_map/ppermute | solution.py:19
  22.5 4.6 copy-start.18
  26.7 14.3 %collective-permute-start.3 = (f32[256,128]{1,0:T(8,128)S(1)}, f32[256,128]{1,0:T(8,128)S(1)}, u32[]{:S(2)}, u32[]{:S(2)}) collective-permute-start(f32[256,128]{1,0:T(8,128)S(1)} %add.107), channel_id=1, source_target_pairs={{0,2},{2,0},{1,3},{3,1},{4,6},{6,4},{5,7},{7,5},{8,10},{10,8},{9,1... | collective-permute-start | bytes 393224 | tf_op jit(solution)/shard_map/ppermute | solution.py:19
  132.5 385.7 %reduce-scatter.4.cloned.1.call-start = ((), (), s32[]{:S(2)}) async-start(), calls=%async_computation.5 | async-start | bytes 7864320 | tf_op jit(solution)/shard_map/reduce_scatter | solution.py:145
  141.9 4.3 copy-start.11
  141.9 4.9 copy-start.14
  141.9 5.5 copy-start.15
  158.5 62.8 %collective-permute-start.4 = (bf16[16,64,3,256]{3,1,2,0:T(8,128)(2,1)}, bf16[16,64,3,256]{3,1,2,0:T(8,128)(2,1)}, u32[]{:S(2)}, u32[]{:S(2)}) collective-permute-start(bf16[16,64,3,256]{3,1,2,0:T(8,128)(2,1)} %get-tuple-element.52), channel_id=1, source_target_pairs={{0,4},{1,5},{2,6},{3,7},{16,20},{17,21},{18,22},{19,23}} | collective-permute-start | bytes 4718600 | tf_op jit(solution)/shard_map/ppermute | solution.py:54
  161.9 68.6 %collective-permute-start.7 = (bf16[16,64,3,256]{3,1,2,0:T(8,128)(2,1)}, bf16[16,64,3,256]{3,1,2,0:T(8,128)(2,1)}, u32[]{:S(2)}, u32[]{:S(2)}) collective-permute-start(bf16[16,64,3,256]{3,1,2,0:T(8,128)(2,1)} %get-tuple-element.53), channel_id=1, source_target_pairs={{12,8},{13,9},{14,10},{15,11},{28,24},{29,25},{30,26},{31,27}} | collective-permute-start | bytes 4718600 | tf_op jit(solution)/shard_map/ppermute | solution.py:57
  225.0 58.3 %collective-permute-start.5 = (bf16[16,64,3,256]{3,1,2,0:T(8,128)(2,1)}, bf16[16,64,3,256]{3,1,2,0:T(8,128)(2,1)}, u32[]{:S(2)}, u32[]{:S(2)}) collective-permute-start(bf16[16,64,3,256]{3,1,2,0:T(8,128)(2,1)} %fusion.22), channel_id=1, source_target_pairs={{0,4},{4,8},{1,5},{5,9},{2,6},{6,10},{3,7},{7,11},{16,20},{20,24},... | collective-permute-start | bytes 4718600 | tf_op jit(solution)/shard_map/ppermute | solution.py:54
  289.4 6.8 %collective-permute-start.8 = (bf16[16,64,3,256]{3,1,2,0:T(8,128)(2,1)}, bf16[16,64,3,256]{3,1,2,0:T(8,128)(2,1)}, u32[]{:S(2)}, u32[]{:S(2)}) collective-permute-start(bf16[16,64,3,256]{3,1,2,0:T(8,128)(2,1)} %get-tuple-element.51), channel_id=1, source_target_pairs={{8,4},{12,8},{9,5},{13,9},{10,6},{14,10},{11,7},{15,11},{24,20},{2... | collective-permute-start | bytes 4718600 | tf_op jit(solution)/shard_map/ppermute | solution.py:57
  291.1 37.2 %collective-permute-start.6 = (bf16[16,64,3,256]{3,1,2,0:T(8,128)(2,1)}, bf16[16,64,3,256]{3,1,2,0:T(8,128)(2,1)}, u32[]{:S(2)}, u32[]{:S(2)}) collective-permute-start(bf16[16,64,3,256]{3,1,2,0:T(8,128)(2,1)} %get-tuple-element.50), channel_id=1, source_target_pairs={{0,4},{4,8},{8,12},{1,5},{5,9},{9,13},{2,6},{6,10},{10,14},{3,7},{... | collective-permute-start | bytes 4718600 | tf_op jit(solution)/shard_map/ppermute | solution.py:54
  299.9 68.4 %collective-permute-start.9 = (bf16[16,64,3,256]{3,1,2,0:T(8,128)(2,1)}, bf16[16,64,3,256]{3,1,2,0:T(8,128)(2,1)}, u32[]{:S(2)}, u32[]{:S(2)}) collective-permute-start(bf16[16,64,3,256]{3,1,2,0:T(8,128)(2,1)} %fusion.21), channel_id=1, source_target_pairs={{4,0},{8,4},{12,8},{5,1},{9,5},{13,9},{6,2},{10,6},{14,10},{7,3},{... | collective-permute-start | bytes 4718600 | tf_op jit(solution)/shard_map/ppermute | solution.py:57
  306.7 66.5 %copy-start.10 = (bf16[256,16,1,256]{3,0,2,1:T(8,128)(2,1)S(1)}, bf16[256,16,1,256]{3,0,2,1:T(8,128)(2,1)}, u32[]{:S(2)}) copy-start(bf16[256,16,1,256]{3,0,2,1:T(8,128)(2,1)} %get-tuple-element.69) | copy-start | bytes 6291460
  381.6 13.0 %slice-start = ((s8[6291456]{0:T(1024)(128)(4,1)}), s8[2097152]{0:T(1024)(128)(4,1)S(1)}, s32[]{:S(2)}) async-start(s8[6291456]{0:T(1024)(128)(4,1)} %bitcast.191), calls=%async_computation.8 | async-start | bytes 4194304
  387.4 7.2 %slice-start.1 = ((s8[6291456]{0:T(1024)(128)(4,1)}), s8[4194304]{0:T(1024)(128)(4,1)S(1)}, s32[]{:S(2)}) async-start(s8[6291456]{0:T(1024)(128)(4,1)} %bitcast.191), calls=%async_computation.9 | async-start | bytes 8388608
  407.6 171.8 %reduce-scatter.6.cloned.1.call-start = ((), (), s32[]{:S(2)}) async-start(), calls=%async_computation.6 | async-start | bytes 655360 | tf_op jit(solution)/shard_map/reduce_scatter | solution.py:184
  410.2 111.5 %copy-start.8 = (bf16[256,2048]{1,0:T(8,128)(2,1)S(1)}, bf16[256,2048]{1,0:T(8,128)(2,1)}, u32[]{:S(2)}) copy-start(bf16[256,2048]{1,0:T(8,128)(2,1)} %param.10) | copy-start | bytes 3145732
  410.2 1.4 collective-permute-start.12
  411.6 5.6 collective-permute-start.13
  522.8 58.3 %reduce-scatter.8.cloned.1.call-start = ((), (), s32[]{:S(2)}) async-start(), calls=%async_computation.7 | async-start | bytes 1310720 | tf_op jit(solution)/shard_map/reduce_scatter | solution.py:196
  533.8 27.6 %collective-permute-start.10 = (bf16[256,2048]{1,0:T(8,128)(2,1)S(1)}, bf16[256,2048]{1,0:T(8,128)(2,1)}, u32[]{:S(2)}, u32[]{:S(2)}) collective-permute-start(bf16[256,2048]{1,0:T(8,128)(2,1)S(1)} %bitcast.212), channel_id=1, source_target_pairs={{0,1},{1,0},{2,3},{3,2},{4,5},{5,4},{6,7},{7,6},{8,9},{9,8},{10,11... | collective-permute-start | bytes 3145736 | tf_op jit(solution)/shard_map/ppermute | solution.py:19
  546.9 25.9 %collective-permute-start.11 = (bf16[256,2048]{1,0:T(8,128)(2,1)}, bf16[256,2048]{1,0:T(8,128)(2,1)}, u32[]{:S(2)}, u32[]{:S(2)}) collective-permute-start(bf16[256,2048]{1,0:T(8,128)(2,1)} %bitcast.100), channel_id=1, source_target_pairs={{0,2},{2,0},{1,3},{3,1},{4,6},{6,4},{5,7},{7,5},{8,10},{10,8},{9,1... | collective-permute-start | bytes 3145736 | tf_op jit(solution)/shard_map/ppermute | solution.py:19
  557.8 15.0 %copy-start.13 = (bf16[128,2048]{1,0:T(8,128)(2,1)S(1)}, bf16[128,2048]{1,0:T(8,128)(2,1)}, u32[]{:S(2)}) copy-start(bf16[128,2048]{1,0:T(8,128)(2,1)} %param.14) | copy-start | bytes 1572868
  561.3 14.7 %copy-start.5 = (f32[64,16,3,256]{3,0,2,1:T(8,128)S(1)}, f32[64,16,3,256]{3,0,2,1:T(8,128)}, u32[]{:S(2)}) copy-start(f32[64,16,3,256]{3,0,2,1:T(8,128)} %convert_bitcast_fusion) | copy-start | bytes 9437188
  572.8 10.1 %copy-start.1 = (bf16[64,16,3,256]{3,1,2,0:T(8,128)(2,1)S(1)}, bf16[64,16,3,256]{3,1,2,0:T(8,128)(2,1)}, u32[]{:S(2)}) copy-start(bf16[64,16,3,256]{3,1,2,0:T(8,128)(2,1)} %param.12) | copy-start | bytes 4718596
  (10 other events, 21.0 us)
Sparse Core Ops, SparseCore 0:
  10.2 101.4 all-gather.2
  132.6 137.7 all-gather.4
  407.8 110.3 reduce-scatter.3
  522.9 22.3 reduce-scatter.5
  547.5 25.5 reduce-scatter.7

commit v4 on v2

--- a/solution.py
+++ b/solution.py
@@ -19,7 +19,7 @@
     return lax.ppermute(block, axis, route)
 
 
-def shared_gather(block):
+def shared_gather(block, after=None):
     group_count = lax.axis_size("groups")
     dp_count = lax.axis_size("dp")
     rows = block.shape[0]
@@ -27,11 +27,14 @@
         return lax.all_gather(block, "dp", axis=0, tiled=True)
     share = rows // group_count
     mine = lax.dynamic_slice_in_dim(block, lax.axis_index("groups") * share, share, axis=0)
-    gathered = lax.all_gather(mine, ("groups", "dp"), axis=0, tiled=True)
-    rest = block.shape[1:]
-    gathered = gathered.reshape((group_count, dp_count, share) + rest)
-    gathered = jnp.swapaxes(gathered, 0, 1)
-    return gathered.reshape((dp_count * rows,) + rest)
+    if after is not None:
+        mine, _ = lax.optimization_barrier((mine, after))
+    return lax.all_gather(mine, ("dp", "groups"), axis=0, tiled=True)
+
+
+def split_rows(values, axis, count):
+    rows = values.shape[axis] // count
+    return [lax.slice_in_dim(values, d * rows, (d + 1) * rows, axis=axis) for d in range(count)]
 
 
 def butterfly_sum(values, axis):
@@ -74,7 +77,8 @@
     blocks_here = width_here // block_size
     dp_size = lax.axis_size("dp")
     inv_root = 1.0 / math.sqrt(tokens_here * dp_size)
-    up_full, down_full = (shared_gather(up_blocks), shared_gather(down_blocks))
+    up_full = shared_gather(up_blocks)
+    down_full = shared_gather(down_blocks)
     sources = [inputs] + [
         swapped(inputs, "tensor", level_bit) for level_bit in range(section_count - 1)
     ]
@@ -90,11 +94,32 @@
     activated, slopes = gelu_pair(preact)
     hidden = activated.astype(jnp.bfloat16)
     picked = pick_blocks([cotangent] * section_count, down_pattern, block_size)
+    hidden_blocks = hidden.reshape(tokens_here, hidden_here, block_size)
+    down_parts = (
+        jnp.stack(
+            [
+                jnp.einsum("thj,thso->hjso", rows, picked, preferred_element_type=jnp.float32)
+                for rows in split_rows(hidden_blocks, 2, dp_size)
+            ]
+        )
+        * inv_root
+    ).astype(jnp.bfloat16)
+    down_parts, down_full = lax.optimization_barrier((down_parts, down_full))
+    grad_down = lax.psum_scatter(
+        down_parts, "dp", scatter_dimension=0, tiled=False
+    ).astype(jnp.float32)
+    grad_down = jnp.transpose(grad_down, (1, 0, 2, 3))
     grad_hidden = jnp.einsum(
         "thso,jhso->thj", picked, down_full, preferred_element_type=jnp.float32
     ).reshape(tokens_here, -1)
     grad_pre = (grad_hidden * slopes).astype(jnp.bfloat16)
     grad_blocks = grad_pre.reshape(tokens_here, hidden_here, block_size)
+    up_parts = jnp.stack(
+        [
+            jnp.einsum("thsi,thj->hsij", rows, grad_blocks, preferred_element_type=jnp.float32)
+            for rows in split_rows(selected, 3, dp_size)
+        ]
+    )
     slot_ids = jnp.arange(blocks_here, dtype=jnp.int32)
 
     def section_term(which_section):
@@ -118,28 +143,12 @@
     grad_input = (
         own_term + jnp.dot(back_low, low_left, preferred_element_type=jnp.float32)
     ).astype(jnp.bfloat16)
-    row_part = selected
+    up_parts, _ = lax.optimization_barrier((up_parts, grad_down))
     grad_up = lax.psum_scatter(
-        (
-            jnp.einsum("thsi,thj->ihsj", row_part, grad_blocks, preferred_element_type=jnp.float32)
-            * inv_root
-        ).astype(jnp.bfloat16),
-        "dp",
-        scatter_dimension=0,
-        tiled=True,
+        (up_parts * inv_root).astype(jnp.bfloat16), "dp", scatter_dimension=0, tiled=False
     ).astype(jnp.float32)
-    hidden_blocks = hidden.reshape(tokens_here, hidden_here, block_size)
-    row_part = hidden_blocks
-    grad_down = lax.psum_scatter(
-        (
-            jnp.einsum("thj,thso->jhso", row_part, picked, preferred_element_type=jnp.float32)
-            * inv_root
-        ).astype(jnp.bfloat16),
-        "dp",
-        scatter_dimension=0,
-        tiled=True,
-    ).astype(jnp.float32)
-    row_part = back_low
+    row_part, low_row_part, grad_up = lax.optimization_barrier((back_low, low_sum, grad_up))
+    grad_up = jnp.transpose(grad_up, (2, 0, 1, 3))
     grad_left = lax.psum_scatter(
         (
             lax.dot_general(
@@ -151,11 +160,10 @@
         scatter_dimension=0,
         tiled=True,
     ).astype(jnp.float32)
-    row_part = low_sum
     grad_right = lax.psum_scatter(
         (
             lax.dot_general(
-                row_part, grad_pre, (((0,), (0,)), ((), ())), preferred_element_type=jnp.float32
+                low_row_part, grad_pre, (((0,), (0,)), ((), ())), preferred_element_type=jnp.float32
             )
             * inv_root
         ).astype(jnp.bfloat16),

time: 543 us -> 530 us (0.976); the launches traced: 542 us -> 521 us
  waiting for transfers between devices: 344 us -> 306 us
  other arithmetic: 23.4 us -> 52.8 us
  local copies, waits for them, and re-layouts: 97.6 us -> 68.4 us
  starting transfers between devices: 6.68 us -> 16.4 us
  matrix products: 55.8 us -> 62.7 us
    all_gather x2, waiting for transfers between devices: 148 us -> 115 us  [shared_gather(): return lax.all_gather(mine, ('dp', 'groups'), axis=0, tiled=True)]
    convert_element_type x2 -> x0, local copies, waits for them, and re-layouts: 18.1 us -> none  [the longest x1 9.06 us: shards(): grad_up = lax.psum_scatter((jnp.einsum('thsi,thj->ihsj', row_part, grad_b...]
    convert_element_type x3 -> x5, other arithmetic: 8.94 us -> 23.6 us  [the longest x1 9.16 us: shards(): (up_parts * inv_root).astype(jnp.bfloat16)]
    reduce_scatter x1, starting transfers between devices: 0.04 us -> 9.23 us  [shards(): lax.psum_scatter((lax.dot_general(row_part, inputs, (((0,), (0,)), ((), (...]
    reduce_scatter x3, waiting for transfers between devices: 172 us -> 164 us  [the longest x1 93.2 us: shards(): lax.psum_scatter((up_parts * inv_root).astype(jnp.bfloat16), 'dp', scatte...]
    another operation x4 -> x5, other arithmetic: 12.8 us -> 19.1 us  [pick_blocks(): return jnp.stack(picked, axis=2)]
    transpose x1 -> x0, local copies, waits for them, and re-layouts: 5.97 us -> none  [shared_gather(): gathered = jnp.swapaxes(gathered, 0, 1)]
    slice x1 -> x0, local copies, waits for them, and re-layouts: 5.5 us -> none  [section_term(): up_full[:, :, which_section, :]]
  transfers between devices with their start and end apart: 14 -> 14, of which waited for: 8 -> 8; matrix products, arithmetic and copies ran while one was open for 23% -> 30% of each run, Pallas kernels for 0% -> 0%
where the time goes in v4:
time: 530 us; the launch traced here: 521 us
  waiting for transfers between devices  306 us (58%)
  local copies, waits for them, and re-layouts  68.4 us (13%)
  matrix products  62.7 us (12%)
  other arithmetic  52.8 us (10%)
  starting transfers between devices  16.4 us (3%)
  between operations  14.7 us (3%)
    all_gather x2, waiting for transfers between devices, shared_gather(): return lax.all_gather(mine, ('dp', 'groups'), axis=0, tiled=True)  115 us
    reduce_scatter x1, waiting for transfers between devices, shards(): lax.psum_scatter((up_parts * inv_root).astype(jnp.bfloat16), 'dp', scatte...  93.2 us
    reduce_scatter x1, waiting for transfers between devices, shards(): lax.psum_scatter(down_parts, 'dp', scatter_dimension=0, tiled=False)  70.9 us
    ppermute x8, waiting for transfers between devices, swapped(): return lax.ppermute(block, axis, route)  26.8 us
    unnamed x53, local copies, waits for them, and re-layouts  20 us
    another operation x5, other arithmetic, pick_blocks(): return jnp.stack(picked, axis=2)  19.1 us
    transpose x3, local copies, waits for them, and re-layouts, section_term(): jnp.einsum('thj,ihj->thi', grad_blocks, up_full[:, :, which_section, :],...  12.5 us
    gather x6, local copies, waits for them, and re-layouts, pick_blocks(): picked.append(jnp.take(shaped, pattern[:, which_section], axis=1))  12.2 us
  transfers between devices with their start and end apart: 14, of which 8 were waited for; matrix products, arithmetic and copies ran while one was open for 30% of the time, Pallas kernels for 0%

profile of v4, /device:TPU:0, one launch (start us, length us, event | category | flops | bytes accessed | tf_op | source)
XLA Modules:
  0.0 521.0 jit_solution(6455031674701592730)
XLA Ops:
  30.5 4.8 select_bitcast_fusion
  39.7 5.4 %collective-permute-done.3 = f32[256,128]{1,0:T(8,128)S(1)} collective-permute-done((f32[256,128]{1,0:T(8,128)S(1)}, f32[256,128]{1,0:T(8,128)S(1)}, u32[]{:S(2)}, u32[]{:S(2)}) %collective-permute-start.3) | collective-permute-done | bytes 131104 | tf_op jit(solution)/shard_map/ppermute | solution.py:19
  52.2 4.0 select_bitcast_fusion.3
  56.2 55.4 %all-gather.3.cloned.1.call-done = bf16[256,16,3,256]{3,0,2,1:T(8,128)(2,1)} async-done(((bf16[32,16,3,256]{3,0,2,1:T(8,128)(2,1)}), bf16[256,16,3,256]{3,0,2,1:T(8,128)(2,1)}) %all-gather.3.cloned.1.call-update) | async-done | bytes 6291472 | tf_op jit(solution)/shard_map/all_gather | solution.py:32
  111.6 8.2 %fusion.52 = f32[16,256,256,1]{2,1,3,0:T(8,128)} fusion(bf16[256,16,3,256]{3,0,2,1:T(8,128)(2,1)} %all-gather.3.cloned.1.call-done, bf16[256,16,1,256]{3,0,2,1:T(8,128)(2,1)S(1)} %get-tuple-element.63, bf16[256,16,1,256]{3,0,2,1:T(8,128)(2,1)} %get-tuple-element.64, bf16[256,16,1,256]{3,0,2,1:T(8,128)(2,1)} %select_bitcast_fusion.5), kind=kOutput, calls=%fused_computation.111 | convolution fusion | flops 1616904192 | bytes 16777216 | tf_op jit(solution)/shard_map/thsi,ihsj->thj/dot_general | solution.py:86
  119.9 5.7 %copy.90 = f32[256,4096]{1,0:T(8,128)} copy(f32[256,4096]{0,1:T(8,128)} %bitcast.188) | data formatting | bytes 8388608 | tf_op jit(solution)/shard_map/reshape | solution.py:91
  125.6 6.9 %multiply_convert_fusion.1 = (bf16[256,4096]{1,0:T(8,128)(2,1)}, f32[256,4096]{1,0:T(8,128)}) fusion(f32[256,4096]{1,0:T(8,128)} %copy.90, bf16[256,128]{1,0:T(8,128)(2,1)S(1)} %add_convert_fusion.2, bf16[128,4096]{1,0:T(8,128)(2,1)} %param.15), kind=kOutput, calls=%fused_computation.26 | convolution fusion | flops 278921216 | bytes 11599872 | tf_op jit(solution)/shard_map/dot_general | solution.py:91
  132.5 4.1 copy.140
  136.7 3.8 convolution_bitcast_fusion.6
  147.0 4.1 fusion
  151.1 59.6 %all-gather.5.cloned.1.call-done = bf16[256,16,3,256]{3,1,2,0:T(8,128)(2,1)} async-done(((bf16[32,16,3,256]{3,1,2,0:T(8,128)(2,1)}), bf16[256,16,3,256]{3,1,2,0:T(8,128)(2,1)}) %all-gather.5.cloned.1.call-update) | async-done | bytes 6291472 | tf_op jit(solution)/shard_map/all_gather | solution.py:32
  211.1 7.0 %pad_maximum_fusion.1 = bf16[256,16,3,256]{3,0,2,1:T(8,128)(2,1)} fusion(bf16[256,16,1,256]{3,0,2,1:T(8,128)(2,1)S(1)} %get-tuple-element.63, bf16[256,16,1,256]{3,0,2,1:T(8,128)(2,1)} %get-tuple-element.64, bf16[256,16,1,256]{3,0,2,1:T(8,128)(2,1)} %select_bitcast_fusion.5), kind=kLoop, calls=%fused_computation.10 | loop fusion | flops 6291456 | bytes 12582912 | tf_op jit(solution)/shard_map/stack | solution.py:67
  218.1 6.3 %fusion.1 = f32[16,256,256,1]{2,1,3,0:T(8,128)} fusion(bf16[256,16,3,256]{3,1,2,0:T(8,128)(2,1)} %all-gather.5.cloned.1.call-done, bf16[256,16,1,256]{3,0,2,1:T(8,128)(2,1)S(1)} %copy-done.10, bf16[256,16,1,256]{3,0,2,1:T(8,128)(2,1)S(1)} %copy-done.12, bf16[256,16,1,256]{3,0,2,1:T(8,128)(2,1)S(1)} %copy-done.16), kind=kOutput, calls=%fused_computation.12 | convolution fusion | flops 1616904192 | bytes 16777216 | tf_op jit(solution)/shard_map/thso,jhso->thj/dot_general | solution.py:112
  224.4 5.8 %copy.131 = f32[256,4096]{1,0:T(8,128)} copy(f32[256,4096]{0,1:T(8,128)} %bitcast.187) | data formatting | bytes 8388608 | tf_op jit(solution)/shard_map/reshape | solution.py:114
  230.1 5.0 fusion.10
  246.2 4.9 pad_maximum_fusion
  251.1 70.9 %reduce-scatter.5.cloned.1.call-done = bf16[1,16,64,3,256]{4,2,3,1,0:T(8,128)(2,1)} async-done(((bf16[4,16,64,3,256]{4,2,3,1,0:T(8,128)(2,1)}), bf16[1,16,64,3,256]{4,2,3,1,0:T(8,128)(2,1)}) %reduce-scatter.5.cloned.1.call-update) | async-done | bytes 1572880 | tf_op jit(solution)/shard_map/reduce_scatter | solution.py:108
  322.0 3.5 convert_bitcast_fusion
  325.5 9.2 %multiply_convert_fusion = bf16[4,16,3,64,256]{4,3,2,1,0:T(8,128)(2,1)} fusion(f32[4,16,3,64,256]{4,3,2,1,0:T(8,128)} %pad_maximum_fusion), kind=kLoop, calls=%fused_computation.9 | loop fusion | flops 6291456 | bytes 18874368 | tf_op jit(solution)/shard_map/convert_element_type | solution.py:148
  334.7 9.2 %reduce-scatter.9.cloned.1.call-start = ((), (), s32[]{:S(2)}) async-start(), calls=%async_computation.8 | async-start | bytes 655360 | tf_op jit(solution)/shard_map/reduce_scatter | solution.py:152
  348.8 4.1 collective-permute-done.7
  352.9 93.2 %reduce-scatter.7.cloned.1.call-done = bf16[1,16,3,64,256]{4,3,2,1,0:T(8,128)(2,1)} async-done(((bf16[4,16,3,64,256]{4,3,2,1,0:T(8,128)(2,1)}), bf16[1,16,3,64,256]{4,3,2,1,0:T(8,128)(2,1)}) %reduce-scatter.7.cloned.1.call-update) | async-done | bytes 1572880 | tf_op jit(solution)/shard_map/reduce_scatter | solution.py:147
  446.1 3.5 bitcast_convert_fusion
  450.8 3.7 convolution_bitcast_fusion.1
  454.5 4.6 copy.104
  463.0 3.7 convolution_bitcast_fusion
  466.7 4.6 copy.106
  476.1 3.7 convolution_bitcast_fusion.2
  479.8 3.3 copy.102
  484.5 16.0 %collective-permute-done.5 = bf16[256,2048]{1,0:T(8,128)(2,1)} collective-permute-done((bf16[256,2048]{1,0:T(8,128)(2,1)}, bf16[256,2048]{1,0:T(8,128)(2,1)}, u32[]{:S(2)}, u32[]{:S(2)}) %collective-permute-start.5) | collective-permute-done | bytes 1048608 | tf_op jit(solution)/shard_map/ppermute | solution.py:19
  503.6 3.5 copy.116
  507.1 3.5 copy.115
  (122 shorter events, 75.1 us)
Async XLA Ops:
  7.2 104.4 %all-gather.3.cloned.1.call-start = ((), (), s32[]{:S(2)}) async-start(), calls=%async_computation.4 | async-start | bytes 7077888 | tf_op jit(solution)/shard_map/all_gather | solution.py:32
  8.6 3.4 copy-start.6
  8.6 7.7 %copy-start.13 = (bf16[128,2048]{1,0:T(8,128)(2,1)S(1)}, bf16[128,2048]{1,0:T(8,128)(2,1)}, u32[]{:S(2)}) copy-start(bf16[128,2048]{1,0:T(8,128)(2,1)} %param.14) | copy-start | bytes 1572868
  9.8 200.9 %all-gather.5.cloned.1.call-start = ((), (), s32[]{:S(2)}) async-start(), calls=%async_computation.5 | async-start | bytes 7077888 | tf_op jit(solution)/shard_map/all_gather | solution.py:32
  12.0 310.0 %reduce-scatter.5.cloned.1.call-start = ((), (), s32[]{:S(2)}) async-start(), calls=%async_computation.6 | async-start | bytes 7864320 | tf_op jit(solution)/shard_map/reduce_scatter | solution.py:108
  13.3 31.8 %collective-permute-start = (bf16[256,2048]{0,1:T(8,128)(2,1)}, bf16[256,2048]{0,1:T(8,128)(2,1)}, u32[]{:S(2)}, u32[]{:S(2)}) collective-permute-start(bf16[256,2048]{0,1:T(8,128)(2,1)} %copy.84), channel_id=1, source_target_pairs={{0,1},{1,0},{2,3},{3,2},{4,5},{5,4},{6,7},{7,6},{8,9},{9,8},{10,11... | collective-permute-start | bytes 3145736 | tf_op jit(solution)/shard_map/ppermute | solution.py:19
  13.8 32.8 %collective-permute-start.1 = (bf16[256,2048]{0,1:T(8,128)(2,1)}, bf16[256,2048]{0,1:T(8,128)(2,1)}, u32[]{:S(2)}, u32[]{:S(2)}) collective-permute-start(bf16[256,2048]{0,1:T(8,128)(2,1)} %copy.84), channel_id=1, source_target_pairs={{0,2},{2,0},{1,3},{3,1},{4,6},{6,4},{5,7},{7,5},{8,10},{10,8},{9,1... | collective-permute-start | bytes 3145736 | tf_op jit(solution)/shard_map/ppermute | solution.py:19
  16.7 22.6 %collective-permute-start.2 = (f32[256,128]{1,0:T(8,128)S(1)}, f32[256,128]{1,0:T(8,128)S(1)}, u32[]{:S(2)}, u32[]{:S(2)}) collective-permute-start(f32[256,128]{1,0:T(8,128)S(1)} %fusion.53), channel_id=1, source_target_pairs={{0,1},{1,0},{2,3},{3,2},{4,5},{5,4},{6,7},{7,6},{8,9},{9,8},{10,11... | collective-permute-start | bytes 393224 | tf_op jit(solution)/shard_map/ppermute | solution.py:19
  17.0 5.3 %copy-start.19 = (s32[16,3]{0,1:T(4,128)S(1)}, s32[16,3]{0,1:T(4,128)}, u32[]{:S(2)}) copy-start(s32[16,3]{0,1:T(4,128)} %param.17) | copy-start | bytes 580
  30.5 4.8 copy-start.8
  39.3 5.8 %collective-permute-start.3 = (f32[256,128]{1,0:T(8,128)S(1)}, f32[256,128]{1,0:T(8,128)S(1)}, u32[]{:S(2)}, u32[]{:S(2)}) collective-permute-start(f32[256,128]{1,0:T(8,128)S(1)} %add.53), channel_id=1, source_target_pairs={{0,2},{2,0},{1,3},{3,1},{4,6},{6,4},{5,7},{7,5},{8,10},{10,8},{9,1... | collective-permute-start | bytes 393224 | tf_op jit(solution)/shard_map/ppermute | solution.py:19
  136.6 3.8 copy-start.9
  136.6 4.3 copy-start.11
  136.7 4.9 copy-start.15
  136.7 5.6 %copy-start.17 = (bf16[256,4096]{0,1:T(8,128)(2,1)S(1)}, bf16[256,4096]{0,1:T(8,128)(2,1)}, u32[]{:S(2)}) copy-start(bf16[256,4096]{0,1:T(8,128)(2,1)} %copy.140) | copy-start | bytes 6291460
  210.7 235.4 %reduce-scatter.7.cloned.1.call-start = ((), (), s32[]{:S(2)}) async-start(), calls=%async_computation.7 | async-start | bytes 7864320 | tf_op jit(solution)/shard_map/reduce_scatter | solution.py:147
  211.0 7.0 %copy-start.10 = (bf16[256,16,1,256]{3,0,2,1:T(8,128)(2,1)S(1)}, bf16[256,16,1,256]{3,0,2,1:T(8,128)(2,1)}, u32[]{:S(2)}) copy-start(bf16[256,16,1,256]{3,0,2,1:T(8,128)(2,1)} %get-tuple-element.65) | copy-start | bytes 6291460
  211.1 7.0 %copy-start.12 = (bf16[256,16,1,256]{3,0,2,1:T(8,128)(2,1)S(1)}, bf16[256,16,1,256]{3,0,2,1:T(8,128)(2,1)}, u32[]{:S(2)}) copy-start(bf16[256,16,1,256]{3,0,2,1:T(8,128)(2,1)} %get-tuple-element.66) | copy-start | bytes 6291460
  211.1 7.0 %copy-start.16 = (bf16[256,16,1,256]{3,0,2,1:T(8,128)(2,1)S(1)}, bf16[256,16,1,256]{3,0,2,1:T(8,128)(2,1)}, u32[]{:S(2)}) copy-start(bf16[256,16,1,256]{3,0,2,1:T(8,128)(2,1)} %select_bitcast_fusion.2) | copy-start | bytes 6291460
  224.4 12.8 %slice-start = ((s8[6291456]{0:T(1024)(128)(4,1)}), s8[2097152]{0:T(1024)(128)(4,1)S(1)}, s32[]{:S(2)}) async-start(s8[6291456]{0:T(1024)(128)(4,1)} %bitcast.174), calls=%async_computation.10 | async-start | bytes 4194304
  230.1 7.0 %slice-start.1 = ((s8[6291456]{0:T(1024)(128)(4,1)}), s8[4194304]{0:T(1024)(128)(4,1)S(1)}, s32[]{:S(2)}) async-start(s8[6291456]{0:T(1024)(128)(4,1)} %bitcast.174), calls=%async_computation.11 | async-start | bytes 8388608
  334.6 9.3 %copy-start.3 = (bf16[256,4096]{1,0:T(8,128)(2,1)S(1)}, bf16[256,4096]{1,0:T(8,128)(2,1)}, u32[]{:S(2)}) copy-start(bf16[256,4096]{1,0:T(8,128)(2,1)} %copy-done.2) | copy-start | bytes 6291460
  334.7 175.9 %reduce-scatter.9.cloned.1.call-start = ((), (), s32[]{:S(2)}) async-start(), calls=%async_computation.8 | async-start | bytes 655360 | tf_op jit(solution)/shard_map/reduce_scatter | solution.py:152
  345.9 1.4 collective-permute-start.6
  347.3 5.6 %collective-permute-start.7 = (f32[256,128]{1,0:T(8,128)S(1)}, f32[256,128]{1,0:T(8,128)S(1)}, u32[]{:S(2)}, u32[]{:S(2)}) collective-permute-start(f32[256,128]{1,0:T(8,128)S(1)} %add.62), channel_id=1, source_target_pairs={{0,2},{2,0},{1,3},{3,1},{4,6},{6,4},{5,7},{7,5},{8,10},{10,8},{9,1... | collective-permute-start | bytes 393224 | tf_op jit(solution)/shard_map/ppermute | solution.py:19
  450.8 61.4 %reduce-scatter.11.cloned.1.call-start = ((), (), s32[]{:S(2)}) async-start(), calls=%async_computation.9 | async-start | bytes 1310720 | tf_op jit(solution)/shard_map/reduce_scatter | solution.py:163
  461.4 23.1 %collective-permute-start.4 = (bf16[256,2048]{1,0:T(8,128)(2,1)S(1)}, bf16[256,2048]{1,0:T(8,128)(2,1)}, u32[]{:S(2)}, u32[]{:S(2)}) collective-permute-start(bf16[256,2048]{1,0:T(8,128)(2,1)S(1)} %bitcast.196), channel_id=1, source_target_pairs={{0,1},{1,0},{2,3},{3,2},{4,5},{5,4},{6,7},{7,6},{8,9},{9,8},{10,11... | collective-permute-start | bytes 3145736 | tf_op jit(solution)/shard_map/ppermute | solution.py:19
  474.6 25.9 %collective-permute-start.5 = (bf16[256,2048]{1,0:T(8,128)(2,1)}, bf16[256,2048]{1,0:T(8,128)(2,1)}, u32[]{:S(2)}, u32[]{:S(2)}) collective-permute-start(bf16[256,2048]{1,0:T(8,128)(2,1)} %bitcast.90), channel_id=1, source_target_pairs={{0,2},{2,0},{1,3},{3,1},{4,6},{6,4},{5,7},{7,5},{8,10},{10,8},{9,1... | collective-permute-start | bytes 3145736 | tf_op jit(solution)/shard_map/ppermute | solution.py:19
  483.6 16.9 %copy-start.14 = (bf16[128,2048]{1,0:T(8,128)(2,1)S(1)}, bf16[128,2048]{1,0:T(8,128)(2,1)}, u32[]{:S(2)}) copy-start(bf16[128,2048]{1,0:T(8,128)(2,1)} %param.14) | copy-start | bytes 1572868
  484.5 19.1 %copy-start.4 = (f32[64,16,3,256]{3,0,2,1:T(8,128)S(1)}, f32[64,16,3,256]{3,0,2,1:T(8,128)}, u32[]{:S(2)}) copy-start(f32[64,16,3,256]{3,0,2,1:T(8,128)} %convert_bitcast_fusion) | copy-start | bytes 9437188
  503.6 3.5 copy-start.5
  507.1 6.9 %copy-start.1 = (bf16[64,16,3,256]{3,1,2,0:T(8,128)(2,1)S(1)}, bf16[64,16,3,256]{3,1,2,0:T(8,128)(2,1)}, u32[]{:S(2)}) copy-start(bf16[64,16,3,256]{3,1,2,0:T(8,128)(2,1)} %param.12) | copy-start | bytes 4718596
  (4 other events, 7.2 us)
Sparse Core Ops, SparseCore 0:
  10.2 101.4 all-gather.2
  113.8 96.8 all-gather.4
  213.0 108.9 reduce-scatter.4
  334.8 111.2 reduce-scatter.6
  450.9 22.3 reduce-scatter.8
  475.4 25.5 reduce-scatter.10
